TPU v7x, 128 devices: a whole 4x4x4 slice. The times are simulated.
128 devices in a mesh: req: 16 (over y, z), mp: 8 (over x, core).
Axes of the slice: x: 4, y: 4, z: 4, core: 2. Of those that a mesh axis runs over, the one named last changes fastest.
Arguments:
- hidden_in: bfloat16 [16384, 2048], P('req', 'mp'), may hold values from -6 to 6
- w_qkv: bfloat16 [3, 2048, 2048], P(None, 'req', 'mp'), may hold values from -0.125 to 0.125
- w_out: bfloat16 [2048, 2048], P('mp', 'req'), may hold values from -0.125 to 0.125
- attn_gain: bfloat16 [2048], replicated, may hold values from 0.099609375 to 1.8984375
- mlp_gain: bfloat16 [2048], replicated, may hold values from 0.099609375 to 1.8984375
- w_gate: bfloat16 [2048, 8192], P('req', 'mp'), may hold values from -0.125 to 0.125
- w_up: bfloat16 [2048, 8192], P('req', 'mp'), may hold values from -0.125 to 0.125
- w_down: bfloat16 [8192, 2048], P('mp', 'req'), may hold values from -0.0625 to 0.0625
- k_cache: bfloat16 [16, 4096, 2048], P('req', None, 'mp'), may hold values from -363 to 363
- v_cache: bfloat16 [16, 4096, 2048], P('req', None, 'mp'), may hold values from -6 to 6
- cache_len: int32 [16], P('req'), may hold values from 256 to 4096, as said below
Outputs:
- hidden_out: bfloat16 [16384, 2048], P('req', 'mp')
- new_keys: bfloat16 [16384, 2048], P('req', 'mp')
- new_values: bfloat16 [16384, 2048], P('req', 'mp')
Inputs may be any that keep to these rules, and one draw needn't show every extreme that they name: Each request uses its first cache_len slots; later slots hold unused data. Some request's cache is full in every draw.
All inputs are finite; a program needn't handle non-finite values.
Results may differ from a plain program's by a relative error of at most 0.02.
Values may be sent and summed in bfloat16 or wider, within the bound.
No kernel may reach another device: no remote copies, remote signals or barrier semaphores. Data moves between devices by JAX's collectives and lax.ppermute only.
A program may use at most 128 MiB of HBM per device.

v0:
```python
import jax
import jax.numpy as jnp
from jax import lax
from jax.sharding import PartitionSpec as P

HD = 64


THETA = 130000.0
EPSILON = 1e-05
NEG_FILL = -1e30


def rms_scale(rows, gain):
    values = rows.astype(jnp.float32)
    meansq = jnp.mean(values * values, axis=-1, keepdims=True)
    return (values * lax.rsqrt(meansq + EPSILON) * gain.astype(jnp.float32)).astype(jnp.bfloat16)


def rotate(tensor, positions):
    half = tensor.shape[-1] // 2
    freq = THETA ** (-(jnp.arange(half, dtype=jnp.float32) * 2.0 / tensor.shape[-1]))
    angle = positions[:, None, None] * freq[None, None, :]
    cosine = jnp.cos(angle)
    sine = jnp.sin(angle)
    first = tensor[..., :half]
    second = tensor[..., half:]
    return jnp.concatenate(
        [first * cosine - second * sine, second * cosine + first * sine], axis=-1
    )


def absorb(carry, queries, keys, values, valid):
    top, total, accum = carry
    scores = jnp.einsum("qhd,khd->hqk", queries, keys, preferred_element_type=jnp.float32) * HD ** (
        -0.5
    )
    scores = jnp.where(valid[None], scores, NEG_FILL)
    new_top = jnp.maximum(top, jnp.max(scores, axis=-1, keepdims=True))
    factor = jnp.exp(top - new_top)
    probs = jnp.where(valid[None], jnp.exp(scores - new_top), 0.0)
    total = total * factor + jnp.sum(probs, axis=-1, keepdims=True)
    accum = accum * factor + jnp.einsum(
        "hqk,khd->hqd", probs.astype(jnp.bfloat16), values, preferred_element_type=jnp.float32
    )
    return (new_top, total, accum)


def on_device(
    hidden_in, w_qkv, w_out, attn_gain, mlp_gain, w_gate, w_up, w_down, k_cache, v_cache, cache_len
):
    new_count = hidden_in.shape[0]
    width = w_qkv.shape[2]
    heads_local = width // HD
    slots = k_cache.shape[1]
    full_rows = lax.all_gather(hidden_in, "mp", axis=1, tiled=True)
    normed = rms_scale(full_rows, attn_gain)
    columns = normed
    projected = jnp.einsum(
        "nd,kdw->knw",
        columns,
        lax.all_gather(w_qkv, "req", axis=1, tiled=True),
        preferred_element_type=jnp.float32,
    )
    length = cache_len[0]
    positions = (length + jnp.arange(new_count, dtype=jnp.int32)).astype(jnp.float32)
    queries = rotate(projected[0].reshape(new_count, heads_local, HD), positions).astype(
        jnp.bfloat16
    )
    fresh_keys = rotate(projected[1].reshape(new_count, heads_local, HD), positions).astype(
        jnp.bfloat16
    )
    fresh_values = projected[2].astype(jnp.bfloat16).reshape(new_count, heads_local, HD)
    rows = jnp.arange(new_count, dtype=jnp.int32)
    causal = rows[:, None] >= rows[None, :]
    start_carry = (
        jnp.full((heads_local, new_count, 1), NEG_FILL, jnp.float32),
        jnp.zeros((heads_local, new_count, 1), jnp.float32),
        jnp.zeros((heads_local, new_count, HD), jnp.float32),
    )
    carry = absorb(start_carry, queries, fresh_keys, fresh_values, causal)
    cache_keys = k_cache[0].reshape(slots, heads_local, HD)
    cache_values = v_cache[0].reshape(slots, heads_local, HD)
    block = min(slots, 512)
    count = (length + block - 1) // block

    def step_block(index, state):
        begin = index * block
        keys = lax.dynamic_slice_in_dim(cache_keys, begin, block, 0)
        values = lax.dynamic_slice_in_dim(cache_values, begin, block, 0)
        valid = (begin + jnp.arange(block, dtype=jnp.int32) < length)[None, :]
        return absorb(state, queries, keys, values, valid)

    top, total, accum = lax.fori_loop(0, count, step_block, carry)
    attn = (accum / total).transpose(1, 0, 2).reshape(new_count, width).astype(jnp.bfloat16)
    partial_value = jnp.dot(
        attn, lax.all_gather(w_out, "req", axis=1, tiled=True), preferred_element_type=jnp.float32
    )
    summed = lax.psum_scatter(
        partial_value.astype(jnp.bfloat16), "mp", scatter_dimension=1, tiled=True
    ).astype(jnp.float32)
    mid_local = (hidden_in.astype(jnp.float32) + summed).astype(jnp.bfloat16)
    mid_full = lax.all_gather(mid_local, "mp", axis=1, tiled=True)
    normed2 = rms_scale(mid_full, mlp_gain)
    columns = normed2
    gate = jnp.dot(
        columns,
        lax.all_gather(w_gate, "req", axis=0, tiled=True),
        preferred_element_type=jnp.float32,
    )
    upper = jnp.dot(
        columns, lax.all_gather(w_up, "req", axis=0, tiled=True), preferred_element_type=jnp.float32
    )
    units = (jax.nn.silu(gate) * upper).astype(jnp.bfloat16)
    terms = jnp.dot(
        units, lax.all_gather(w_down, "req", axis=1, tiled=True), preferred_element_type=jnp.float32
    )
    reduced = lax.psum_scatter(
        terms.astype(jnp.bfloat16), "mp", scatter_dimension=1, tiled=True
    ).astype(jnp.float32)
    hidden_out = (mid_local.astype(jnp.float32) + reduced).astype(jnp.bfloat16)
    return (
        hidden_out,
        fresh_keys.reshape(new_count, width),
        fresh_values.reshape(new_count, width),
    )


def solution(mesh):
    return jax.shard_map(
        on_device,
        mesh=mesh,
        in_specs=(
            P("req", "mp"),
            P(None, "req", "mp"),
            P("mp", "req"),
            P(),
            P(),
            P("req", "mp"),
            P("req", "mp"),
            P("mp", "req"),
            P("req", None, "mp"),
            P("req", None, "mp"),
            P("req"),
        ),
        out_specs=(P("req", "mp"), P("req", "mp"), P("req", "mp")),
        check_vma=False,
    )
```

profile of v0, /device:TPU:0, one launch (start us, length us, event | category | flops | bytes accessed | tf_op | source)
XLA Modules:
  0.0 498.7 jit_solution(9587442802145398446)
XLA Ops:
  7.2 0.7 all-gather.8.cloned.1.call-update
  7.9 1.7 copy.15
  9.7 0.0 all-gather.12.cloned.1.call-start
  9.8 0.7 all-gather.12.cloned.1.call-update
  10.5 1.3 iota_compare_fusion
  12.4 0.7 convert_element_type.87
  13.1 2.9 copy.17
  16.1 4.2 copy.18
  20.2 0.5 multiply_cosine_fusion
  20.8 27.4 %all-gather.8.cloned.1.call-done = bf16[1024,2048]{1,0:T(8,128)(2,1)} async-done(((bf16[1024,256]{1,0:T(8,128)(2,1)}), bf16[1024,2048]{1,0:T(8,128)(2,1)}) %all-gather.8.cloned.1.call-update) | async-done | bytes 4194320 | tf_op jit(solution)/shard_map/all_gather | solution.py:56
  48.2 3.1 fusion.23
  51.3 53.4 %all-gather.10.cloned.1.call-done = bf16[3,2048,256]{1,2,0:T(8,128)(2,1)} async-done(((bf16[3,128,256]{1,2,0:T(8,128)(2,1)}), bf16[3,2048,256]{1,2,0:T(8,128)(2,1)}) %all-gather.10.cloned.1.call-update) | async-done | bytes 3145744 | tf_op jit(solution)/shard_map/all_gather | solution.py:62
  104.7 6.6 %fusion.37 = f32[3,1024,256]{1,2,0:T(8,128)S(1)} fusion(bf16[3,2048,256]{1,2,0:T(8,128)(2,1)} %all-gather.10.cloned.1.call-done, bf16[1024,2048]{1,0:T(8,128)(2,1)} %all-gather.8.cloned.1.call-done, f32[2048]{0:T(1024)S(1)} %convert_element_type.87, f32[1024]{0:T(1024)S(1)} %add_rsqrt_fusion.1), kind=kOutput, calls=%fused_computation.49 | convolution fusion | flops 3229614080 | bytes 10498048 | tf_op jit(solution)/shard_map/nd,kdw->knw/dot_general | solution.py:59
  111.3 0.2 fusion.54
  111.6 0.1 slice.44
  111.6 0.2 subtract_convert_fusion
  111.8 0.2 multiply_subtract_fusion
  112.0 1.0 copy-done.2
  113.0 0.3 copy-done.1
  113.3 3.0 fusion.20
  116.4 4.2 fusion.22
  120.6 5.9 %fusion.40 = f32[4,1024,64]{1,2,0:T(8,128)} fusion(bf16[1024,4,64]{0,2,1:T(8,128)(2,1)S(1)} %bitcast.80, f32[4,1024,1024]{1,2,0:T(8,128)S(1)} %get-tuple-element.91, f32[4,1024]{1,0:T(4,128)S(1)} %get-tuple-element.87, pred[1024,1024]{0,1:T(8,128)(4,1)S(1)} %copy-done.1, f32[4,1024]{1,0:T(4,128)S(1)} %get-tuple-element.85), kind=kOutput, calls=%fused_computation.50 | convolution fusion | flops 558104576 | bytes 19431424 | tf_op jit(solution)/shard_map/hqk,khd->hqd/dot_general | solution.py:43
  126.5 40.4 %while.14 = (s32[]{:T(128)}, f32[4,1024,1]{1,0,2:T(4,128)S(1)}, f32[4,1024,1]{1,0,2:T(4,128)S(1)}, f32[4,1024,64]{1,2,0:T(8,128)}, s32[]{:T(128)}, /*index=5*/s3...) while((s32[]{:T(128)}, f32[4,1024,1]{1,0,2:T(4,128)S(1)}, ...), condition=%wide.region_6.7_spmd, body=%wide.region_3.6_spmd.sunk | while | flops 564671488 | bytes 36965104 | solution.py:94
  126.5 0.7 add_compare_fusion.2
  127.3 1.6 bitcast_reduce_fusion.2
  128.9 3.1 fusion.74
  132.0 2.5 fusion.73
  134.6 0.7 add_compare_fusion.2
  135.4 1.6 bitcast_reduce_fusion.2
  137.0 3.1 fusion.74
  140.1 2.5 fusion.73
  142.7 0.7 add_compare_fusion.2
  143.4 1.6 bitcast_reduce_fusion.2
  145.1 3.1 fusion.74
  148.1 2.5 fusion.73
  150.8 0.7 add_compare_fusion.2
  151.5 1.6 bitcast_reduce_fusion.2
  153.1 3.1 fusion.74
  156.2 2.5 fusion.73
  158.9 0.7 add_compare_fusion.2
  159.6 1.6 bitcast_reduce_fusion.2
  161.2 3.1 fusion.74
  164.3 2.5 fusion.73
  166.9 1.4 divide_convert_fusion
  168.3 4.5 convolution_convert_fusion
  172.8 0.0 all-gather.14.cloned.1.call-start
  172.9 60.0 %reduce-scatter.3.cloned.1.call-done = bf16[1024,256]{1,0:T(8,128)(2,1)} async-done(((bf16[1024,2048]{1,0:T(8,128)(2,1)}), bf16[1024,256]{1,0:T(8,128)(2,1)}) %reduce-scatter.3.cloned.1.call-update) | async-done | bytes 524304 | tf_op jit(solution)/shard_map/reduce_scatter | solution.py:99
  232.9 2.0 add_convert_fusion.1
  234.9 0.5 all-gather.16.cloned.1.call-update
  235.5 0.7 all-gather.18.cloned.1.call-update
  236.3 0.7 all-gather.20.cloned.1.call-update
  237.0 0.3 reduce-scatter.5.cloned.1.call-start
  237.2 32.8 %all-gather.14.cloned.1.call-done = bf16[1024,2048]{1,0:T(8,128)(2,1)} async-done(((bf16[1024,256]{1,0:T(8,128)(2,1)}), bf16[1024,2048]{1,0:T(8,128)(2,1)}) %all-gather.14.cloned.1.call-update) | async-done | bytes 4194320 | tf_op jit(solution)/shard_map/all_gather | solution.py:103
  270.0 3.1 fusion.26
  273.1 51.6 %all-gather.16.cloned.1.call-done = bf16[2048,1024]{1,0:T(8,128)(2,1)} async-done(((bf16[128,1024]{1,0:T(8,128)(2,1)}), bf16[2048,1024]{1,0:T(8,128)(2,1)}) %all-gather.16.cloned.1.call-update) | async-done | bytes 4194320 | tf_op jit(solution)/shard_map/all_gather | solution.py:108
  324.7 10.0 %fusion.44 = f32[1024,1024]{1,0:T(8,128)} fusion(bf16[2048,1024]{1,0:T(8,128)(2,1)} %all-gather.16.cloned.1.call-done, bf16[1024,2048]{1,0:T(8,128)(2,1)} %all-gather.14.cloned.1.call-done, f32[2048]{0:T(1024)S(1)} %convert_element_type.102, f32[1024]{0:T(1024)S(1)} %add_rsqrt_fusion), kind=kOutput, calls=%fused_computation.51 | convolution fusion | flops 4303355904 | bytes 12595200 | tf_op jit(solution)/shard_map/dot_general | solution.py:106
  334.7 43.5 %all-gather.18.cloned.1.call-done = bf16[2048,1024]{1,0:T(8,128)(2,1)} async-done(((bf16[128,1024]{1,0:T(8,128)(2,1)}), bf16[2048,1024]{1,0:T(8,128)(2,1)}) %all-gather.18.cloned.1.call-update) | async-done | bytes 4194320 | tf_op jit(solution)/shard_map/all_gather | solution.py:112
  378.1 59.4 %all-gather.20.cloned.1.call-done = bf16[1024,2048]{1,0:T(8,128)(2,1)} async-done(((bf16[1024,128]{1,0:T(8,128)(2,1)}), bf16[1024,2048]{1,0:T(8,128)(2,1)}) %all-gather.20.cloned.1.call-update) | async-done | bytes 4194320 | tf_op jit(solution)/shard_map/all_gather | solution.py:116
  437.6 15.4 %convolution_convert_fusion.1 = bf16[1024,2048]{1,0:T(8,128)(2,1)} fusion(bf16[1024,2048]{1,0:T(8,128)(2,1)} %all-gather.20.cloned.1.call-done, f32[1024,1024]{1,0:T(8,128)} %fusion.44, bf16[2048,1024]{1,0:T(8,128)(2,1)} %all-gather.18.cloned.1.call-done, bf16[1024,2048]{1,0:T(8,128)(2,1)} %all-gather.14.cloned.1.call-done, ...), kind=kOutput, calls=%fused_computation.48 | convolution fusion | flops 8606711808 | bytes 20983808 | tf_op jit(solution)/shard_map/dot_general | solution.py:115
  453.0 1.0 copy.19
  454.0 1.3 slice_bitcast_fusion
  455.3 1.0 copy.20
  456.3 33.9 %reduce-scatter.5.cloned.1.call-done = bf16[1024,256]{1,0:T(8,128)(2,1)} async-done(((bf16[1024,2048]{1,0:T(8,128)(2,1)}), bf16[1024,256]{1,0:T(8,128)(2,1)}) %reduce-scatter.5.cloned.1.call-update) | async-done | bytes 524304 | tf_op jit(solution)/shard_map/reduce_scatter | solution.py:118
  490.3 2.0 add_convert_fusion
  (63 shorter events, 0.7 us)
Async XLA Ops:
  7.2 41.0 %all-gather.8.cloned.1.call-start = ((), (), s32[]{:S(2)}) async-start(), calls=%async_computation.2 | async-start | bytes 4718592 | tf_op jit(solution)/shard_map/all_gather | solution.py:56
  7.9 96.8 %all-gather.10.cloned.1.call-start = ((), (), s32[]{:S(2)}) async-start(), calls=%async_computation.3 | async-start | bytes 3342336 | tf_op jit(solution)/shard_map/all_gather | solution.py:62
  9.7 158.6 %all-gather.12.cloned.1.call-start = ((), (), s32[]{:S(2)}) async-start(), calls=%async_computation.4 | async-start | bytes 1114112 | tf_op jit(solution)/shard_map/all_gather | solution.py:97
  10.4 222.4 %reduce-scatter.3.cloned.1.call-start = ((), (), s32[]{:S(2)}) async-start(), calls=%async_computation.5 | async-start | bytes 4718592 | tf_op jit(solution)/shard_map/reduce_scatter | solution.py:99
  111.3 1.7 copy-start.2
  111.3 2.0 copy-start.1
  126.5 2.4 copy-start.4
  132.0 2.6 copy-start.5
  134.6 2.4 copy-start.4
  140.0 2.6 copy-start.5
  142.7 2.4 copy-start.4
  148.1 2.6 copy-start.5
  150.8 2.4 copy-start.4
  156.2 2.6 copy-start.5
  158.8 2.4 copy-start.4
  164.3 2.6 copy-start.5
  166.9 66.0 %copy-start.3 = (bf16[1024,256]{1,0:T(8,128)(2,1)S(1)}, bf16[1024,256]{1,0:T(8,128)(2,1)}, u32[]{:S(2)}) copy-start(bf16[1024,256]{1,0:T(8,128)(2,1)} %param.13) | copy-start | bytes 1572868
  166.9 70.3 %copy-start.6 = (bf16[2048]{0:T(1024)(128)(2,1)S(1)}, bf16[2048]{0:T(1024)(128)(2,1)}, u32[]{:S(2)}) copy-start(bf16[2048]{0:T(1024)(128)(2,1)} %param.17) | copy-start | bytes 12292
  172.8 97.2 %all-gather.14.cloned.1.call-start = ((), (), s32[]{:S(2)}) async-start(), calls=%async_computation.6 | async-start | bytes 4718592 | tf_op jit(solution)/shard_map/all_gather | solution.py:103
  234.9 89.8 %all-gather.16.cloned.1.call-start = ((), (), s32[]{:S(2)}) async-start(), calls=%async_computation.7 | async-start | bytes 4456448 | tf_op jit(solution)/shard_map/all_gather | solution.py:108
  235.5 142.7 %all-gather.18.cloned.1.call-start = ((), (), s32[]{:S(2)}) async-start(), calls=%async_computation.8 | async-start | bytes 4456448 | tf_op jit(solution)/shard_map/all_gather | solution.py:112
  236.2 201.4 %all-gather.20.cloned.1.call-start = ((), (), s32[]{:S(2)}) async-start(), calls=%async_computation.9 | async-start | bytes 4456448 | tf_op jit(solution)/shard_map/all_gather | solution.py:116
  237.0 253.3 %reduce-scatter.5.cloned.1.call-start = ((), (), s32[]{:S(2)}) async-start(), calls=%async_computation.10 | async-start | bytes 4718592 | tf_op jit(solution)/shard_map/reduce_scatter | solution.py:118
  453.0 37.3 %copy-start = (bf16[1024,256]{1,0:T(8,128)(2,1)S(1)}, bf16[1024,256]{1,0:T(8,128)(2,1)}, u32[]{:S(2)}) copy-start(bf16[1024,256]{1,0:T(8,128)(2,1)} %add_convert_fusion.1) | copy-start | bytes 1572868
Sparse Core Ops, SparseCore 0:
  9.7 38.4 all-gather.7
  50.9 53.7 all-gather.9
  106.8 42.7 all-gather.11
  173.0 59.8 reduce-scatter.2
  235.0 34.9 all-gather.13
  272.0 52.6 all-gather.15
  326.9 51.2 all-gather.17
  380.2 57.2 all-gather.19
  453.1 37.0 reduce-scatter.4
where the time goes:
time: 500 us; the launch traced here: 499 us
  waiting for transfers between devices  365 us (73%)
  matrix products  68.6 us (14%)
  other arithmetic  35.2 us (7%)
  between operations  14.7 us (3%)
  local copies, waits for them, and re-layouts  13.8 us (3%)
    reduce_scatter x1, waiting for transfers between devices, on_device(): lax.psum_scatter(partial_value.astype(jnp.bfloat16), 'mp', scatter_dimens...  60 us
    all_gather x1, waiting for transfers between devices, on_device(): lax.all_gather(w_down, 'req', axis=1, tiled=True)  59.4 us
    all_gather x1, waiting for transfers between devices, on_device(): lax.all_gather(w_qkv, 'req', axis=1, tiled=True)  53.4 us
    all_gather x1, waiting for transfers between devices, on_device(): lax.all_gather(w_gate, 'req', axis=0, tiled=True)  51.6 us
    all_gather x1, waiting for transfers between devices, on_device(): lax.all_gather(w_up, 'req', axis=0, tiled=True)  43.5 us
    reduce_scatter x1, waiting for transfers between devices, on_device(): lax.psum_scatter(terms.astype(jnp.bfloat16), 'mp', scatter_dimension=1, t...  33.9 us
    all_gather x1, waiting for transfers between devices, on_device(): mid_full = lax.all_gather(mid_local, 'mp', axis=1, tiled=True)  32.8 us
    all_gather x1, waiting for transfers between devices, on_device(): full_rows = lax.all_gather(hidden_in, 'mp', axis=1, tiled=True)  27.4 us
  transfers between devices with their start and end apart: 9, of which 8 were waited for; matrix products, arithmetic and copies ran while one was open for 19% of the time, Pallas kernels for 0%

commit v1 on v0

--- a/solution.py
+++ b/solution.py
@@ -30,6 +30,33 @@
     )
 
 
+def _side(n):
+    side = int(round(n ** 0.5))
+    return side if side * side == n else 1
+
+
+def gather_req(block, axis, n_req):
+    side_z = _side(n_req)
+    side_y = n_req // side_z
+    me = lax.axis_index("req")
+    row, col = me // side_z, me % side_z
+
+    def shift_z(k):
+        return [(s, (s // side_z) * side_z + (s % side_z - k) % side_z) for s in range(n_req)]
+
+    def shift_y(k):
+        return [(s, ((s // side_z - k) % side_y) * side_z + s % side_z) for s in range(n_req)]
+
+    parts = [block] + [lax.ppermute(block, "req", shift_z(k)) for k in range(1, side_z)]
+    stage = jnp.stack(parts, axis=axis)
+    parts = [stage] + [lax.ppermute(stage, "req", shift_y(k)) for k in range(1, side_y)]
+    full = jnp.stack(parts, axis=axis)
+    full = jnp.roll(full, (row, col), axis=(axis, axis + 1))
+    shape = list(block.shape)
+    shape[axis] *= n_req
+    return full.reshape(shape)
+
+
 def absorb(carry, queries, keys, values, valid):
     top, total, accum = carry
     scores = jnp.einsum("qhd,khd->hqk", queries, keys, preferred_element_type=jnp.float32) * HD ** (
@@ -50,6 +77,12 @@
     hidden_in, w_qkv, w_out, attn_gain, mlp_gain, w_gate, w_up, w_down, k_cache, v_cache, cache_len
 ):
     new_count = hidden_in.shape[0]
+    n_req = lax.axis_size("req")
+    w_qkv_full = gather_req(w_qkv, 1, n_req)
+    out_rows = w_out.shape[0]
+    out_down = gather_req(jnp.concatenate([w_out, w_down], axis=0), 1, n_req)
+    w_out_full, w_down_full = out_down[:out_rows], out_down[out_rows:]
+    gate_up = gather_req(jnp.stack([w_gate, w_up]), 1, n_req)
     width = w_qkv.shape[2]
     heads_local = width // HD
     slots = k_cache.shape[1]
@@ -59,7 +92,7 @@
     projected = jnp.einsum(
         "nd,kdw->knw",
         columns,
-        lax.all_gather(w_qkv, "req", axis=1, tiled=True),
+        w_qkv_full,
         preferred_element_type=jnp.float32,
     )
     length = cache_len[0]
@@ -94,7 +127,7 @@
     top, total, accum = lax.fori_loop(0, count, step_block, carry)
     attn = (accum / total).transpose(1, 0, 2).reshape(new_count, width).astype(jnp.bfloat16)
     partial_value = jnp.dot(
-        attn, lax.all_gather(w_out, "req", axis=1, tiled=True), preferred_element_type=jnp.float32
+        attn, w_out_full, preferred_element_type=jnp.float32
     )
     summed = lax.psum_scatter(
         partial_value.astype(jnp.bfloat16), "mp", scatter_dimension=1, tiled=True
@@ -105,15 +138,15 @@
     columns = normed2
     gate = jnp.dot(
         columns,
-        lax.all_gather(w_gate, "req", axis=0, tiled=True),
+        gate_up[0],
         preferred_element_type=jnp.float32,
     )
     upper = jnp.dot(
-        columns, lax.all_gather(w_up, "req", axis=0, tiled=True), preferred_element_type=jnp.float32
+        columns, gate_up[1], preferred_element_type=jnp.float32
     )
     units = (jax.nn.silu(gate) * upper).astype(jnp.bfloat16)
     terms = jnp.dot(
-        units, lax.all_gather(w_down, "req", axis=1, tiled=True), preferred_element_type=jnp.float32
+        units, w_down_full, preferred_element_type=jnp.float32
     )
     reduced = lax.psum_scatter(
         terms.astype(jnp.bfloat16), "mp", scatter_dimension=1, tiled=True

time: 500 us -> 519 us (1.038); the launches traced: 499 us -> 513 us
  waiting for transfers between devices: 365 us -> 290 us
  local copies, waits for them, and re-layouts: 13.8 us -> 70.3 us
  starting transfers between devices: 0.57 us -> 31.1 us
  other arithmetic: 35.2 us -> 48 us
  matrix products: 68.6 us -> 57.4 us
    all_gather x5 -> x0, waiting for transfers between devices: 208 us -> none  [the longest x1 59.4 us: on_device(): lax.all_gather(w_down, 'req', axis=1, tiled=True)]
    ppermute x0 -> x18, waiting for transfers between devices: none -> 174 us  [the longest x9 148 us: gather_req(): lax.ppermute(stage, 'req', shift_y(k))]
    all_gather x1, waiting for transfers between devices: 32.8 us -> 0.01 us  [on_device(): mid_full = lax.all_gather(mid_local, 'mp', axis=1, tiled=True)]
    ppermute x0 -> x18, starting transfers between devices: none -> 30.9 us  [the longest x9 17.6 us: gather_req(): lax.ppermute(block, 'req', shift_z(k))]
    all_gather x1, waiting for transfers between devices: 27.4 us -> 0.02 us  [on_device(): full_rows = lax.all_gather(hidden_in, 'mp', axis=1, tiled=True)]
    unnamed x15 -> x65, local copies, waits for them, and re-layouts: 12.2 us -> 36.3 us
    reduce_scatter x1, waiting for transfers between devices: 60 us -> 78.5 us  [on_device(): lax.psum_scatter(partial_value.astype(jnp.bfloat16), 'mp', scatter_dimens...]
    dynamic_slice x0 -> x4, local copies, waits for them, and re-layouts: none -> 15.9 us  [gather_req(): full = jnp.roll(full, (row, col), axis=(axis, axis + 1))]
  transfers between devices with their start and end apart: 9 -> 22, of which waited for: 8 -> 11; matrix products, arithmetic and copies ran while one was open for 19% -> 17% of each run, Pallas kernels for 0% -> 0%
where the time goes in v1:
time: 519 us; the launch traced here: 513 us
  waiting for transfers between devices  290 us (56%)
  local copies, waits for them, and re-layouts  70.3 us (14%)
  matrix products  57.4 us (11%)
  other arithmetic  48 us (9%)
  starting transfers between devices  31.1 us (6%)
  between operations  15.4 us (3%)
    ppermute x9, waiting for transfers between devices, gather_req(): lax.ppermute(stage, 'req', shift_y(k))  148 us
    reduce_scatter x1, waiting for transfers between devices, on_device(): lax.psum_scatter(partial_value.astype(jnp.bfloat16), 'mp', scatter_dimens...  78.5 us
    reduce_scatter x1, waiting for transfers between devices, on_device(): lax.psum_scatter(terms.astype(jnp.bfloat16), 'mp', scatter_dimension=1, t...  37.6 us
    unnamed x65, local copies, waits for them, and re-layouts  36.3 us
    ppermute x9, waiting for transfers between devices, gather_req(): lax.ppermute(block, 'req', shift_z(k))  25.8 us
    ppermute x9, starting transfers between devices, gather_req(): lax.ppermute(block, 'req', shift_z(k))  17.6 us
    dynamic_slice x4, local copies, waits for them, and re-layouts, gather_req(): full = jnp.roll(full, (row, col), axis=(axis, axis + 1))  15.9 us
    dot_general x1, matrix products, on_device(): terms = jnp.dot(units, w_down_full, preferred_element_type=jnp.float32)  15.3 us
  transfers between devices with their start and end apart: 22, of which 11 were waited for; matrix products, arithmetic and copies ran while one was open for 17% of the time, Pallas kernels for 0%

profile of v1, /device:TPU:0, one launch (start us, length us, event | category | flops | bytes accessed | tf_op | source)
XLA Modules:
  0.0 512.5 jit_solution(4735026822149209426)
XLA Ops:
  10.2 2.0 collective-permute-start.8
  12.2 3.6 collective-permute-start.7
  15.8 2.5 collective-permute-start.1
  20.5 4.1 copy.24
  24.6 3.0 copy.25
  28.8 4.6 collective-permute-done.2
  33.4 2.9 collective-permute-start.6
  36.4 2.6 collective-permute-done.1
  40.1 3.1 collective-permute-start.3
  48.5 2.3 collective-permute-start.9
  50.8 1.7 collective-permute-start.10
  53.7 24.4 %collective-permute-done.3 = bf16[3,4,128,256]{3,2,0,1:T(8,128)(2,1)S(1)} collective-permute-done((bf16[3,4,128,256]{3,2,0,1:T(8,128)(2,1)S(1)}, bf16[3,4,128,256]{3,2,0,1:T(8,128)(2,1)S(1)}, u32[]{:S(2)}, u32[]{:S(2)}) %collective-permute-start.3) | collective-permute-done | bytes 786464 | tf_op jit(solution)/shard_map/ppermute | solution.py:52
  78.2 5.2 %collective-permute-done.5 = bf16[3,4,128,256]{3,2,0,1:T(8,128)(2,1)S(1)} collective-permute-done((bf16[3,4,128,256]{3,2,0,1:T(8,128)(2,1)S(1)}, bf16[3,4,128,256]{3,2,0,1:T(8,128)(2,1)S(1)}, u32[]{:S(2)}, u32[]{:S(2)}) %collective-permute-start.5) | collective-permute-done | bytes 786464 | tf_op jit(solution)/shard_map/ppermute | solution.py:52
  86.1 4.6 copy.22
  90.7 6.2 %reshape.166 = bf16[3,2048,256]{1,2,0:T(8,128)(2,1)} reshape(bf16[3,4,4,128,256]{3,2,1,4,0:T(4,128)(2,1)} %copy.22) | data formatting | bytes 6291456 | tf_op jit(solution)/shard_map/reshape | solution.py:57
  96.9 35.4 %collective-permute-done.9 = bf16[1280,4,128]{0,2,1:T(8,128)(2,1)} collective-permute-done((bf16[1280,4,128]{0,2,1:T(8,128)(2,1)}, bf16[1280,4,128]{0,2,1:T(8,128)(2,1)}, u32[]{:S(2)}, u32[]{:S(2)}) %collective-permute-start.9) | collective-permute-done | bytes 1310752 | tf_op jit(solution)/shard_map/ppermute | solution.py:52
  132.3 2.5 bitcast_dynamic-update-slice_fusion.12
  134.7 2.5 bitcast_dynamic-update-slice_fusion.10
  137.2 2.5 bitcast_dynamic-update-slice_fusion.8
  140.9 2.5 bitcast_dynamic-update-slice_fusion.13
  143.4 2.6 bitcast_dynamic-update-slice_fusion.11
  146.0 2.5 bitcast_dynamic-update-slice_fusion.9
  148.4 2.8 constant_dynamic-slice_fusion.1
  151.3 1.9 fusion.33
  153.2 2.3 copy-done
  155.6 3.2 fusion.23
  159.0 5.5 %fusion.40 = f32[3,1024,256]{1,2,0:T(8,128)S(1)} fusion(bf16[3,2048,256]{1,2,0:T(8,128)(2,1)} %reshape.166, bf16[1024,2048]{1,0:T(8,128)(2,1)S(1)} %copy-done.3, f32[2048]{0:T(1024)S(1)} %convert_element_type.87, f32[1024]{0:T(1024)S(1)} %add_rsqrt_fusion.1), kind=kOutput, calls=%fused_computation.67 | convolution fusion | flops 3229614080 | bytes 10498048 | tf_op jit(solution)/shard_map/nd,kdw->knw/dot_general | solution.py:92
  167.0 3.0 fusion.20
  170.1 4.4 fusion.22
  174.5 4.8 fusion.43
  179.3 26.9 %while.14 = (s32[]{:T(128)}, f32[4,1024,1]{1,0,2:T(4,128)S(1)}, f32[4,1024,1]{1,0,2:T(4,128)S(1)}, f32[4,1024,64]{1,2,0:T(8,128)S(1)}, s32[]{:T(128)}, /*index=5...) while((s32[]{:T(128)}, f32[4,1024,1]{1,0,2:T(4,128)S(1)}, ...), condition=%wide.region_6.7_spmd, body=%wide.region_3.6_spmd.sunk | while | flops 564671488 | bytes 28576452 | solution.py:127
  180.0 2.6 bitcast_reduce_fusion.2
  182.6 2.5 fusion.79
  185.2 3.1 fusion.80
  188.9 2.6 bitcast_reduce_fusion.2
  191.5 2.5 fusion.79
  194.1 3.1 fusion.80
  197.9 2.6 bitcast_reduce_fusion.2
  200.5 2.5 fusion.79
  203.1 3.1 fusion.80
  206.3 3.3 convolution_convert_fusion
  209.7 78.5 %reduce-scatter.3.cloned.1.call-done = bf16[1024,256]{1,0:T(8,128)(2,1)} async-done(((bf16[1024,2048]{1,0:T(8,128)(2,1)}), bf16[1024,256]{1,0:T(8,128)(2,1)}) %reduce-scatter.3.cloned.1.call-update) | async-done | bytes 524304 | tf_op jit(solution)/shard_map/reduce_scatter | solution.py:132
  288.1 2.1 add_convert_fusion.1
  290.4 1.6 collective-permute-start.14
  292.0 2.8 collective-permute-start.13
  296.2 9.1 %collective-permute-done.14 = bf16[2,128,1024]{2,1,0:T(8,128)(2,1)S(1)} collective-permute-done((bf16[2,128,1024]{2,1,0:T(8,128)(2,1)S(1)}, bf16[2,128,1024]{2,1,0:T(8,128)(2,1)S(1)}, u32[]{:S(2)}, u32[]{:S(2)}) %collective-permute-start.14) | collective-permute-done | bytes 524320 | tf_op jit(solution)/shard_map/ppermute | solution.py:50
  305.3 9.5 %collective-permute-done.13 = bf16[2,128,1024]{2,1,0:T(8,128)(2,1)S(1)} collective-permute-done((bf16[2,128,1024]{2,1,0:T(8,128)(2,1)S(1)}, bf16[2,128,1024]{2,1,0:T(8,128)(2,1)S(1)}, u32[]{:S(2)}, u32[]{:S(2)}) %collective-permute-start.13) | collective-permute-done | bytes 524320 | tf_op jit(solution)/shard_map/ppermute | solution.py:50
  315.1 2.8 collective-permute-start.15
  319.7 1.5 bitcast_dynamic-update-slice_fusion.6
  321.2 2.5 slice.64
  323.8 82.6 %collective-permute-done.15 = bf16[2,4,128,1024]{3,2,0,1:T(8,128)(2,1)S(1)} collective-permute-done((bf16[2,4,128,1024]{3,2,0,1:T(8,128)(2,1)S(1)}, bf16[2,4,128,1024]{3,2,0,1:T(8,128)(2,1)S(1)}, u32[]{:S(2)}, u32[]{:S(2)}) %collective-permute-start.15) | collective-permute-done | bytes 2097184 | tf_op jit(solution)/shard_map/ppermute | solution.py:52
  406.3 1.5 bitcast_dynamic-update-slice_fusion.4
  407.8 1.5 bitcast_dynamic-update-slice_fusion.2
  410.0 1.6 bitcast_dynamic-update-slice_fusion
  411.6 1.5 bitcast_dynamic-update-slice_fusion.7
  413.1 1.6 bitcast_dynamic-update-slice_fusion.5
  417.6 8.3 %constant_dynamic-slice_fusion = bf16[2,4,4,128,1024]{4,3,0,2,1:T(8,128)(2,1)} fusion(bf16[2,8,4,128,1024]{4,3,0,2,1:T(8,128)(2,1)} %bitcast_dynamic-update-slice_fusion.1, s32[]{:T(128)S(6)} %select_n.89), kind=kLoop, calls=%fused_computation.108 | loop fusion | bytes 16777220 | tf_op jit(solution)/shard_map/jit(_roll_dynamic)/dynamic_slice | solution.py:54
  425.9 5.6 %fusion.29 = bf16[2,4,4,128,1024]{4,3,0,2,1:T(8,128)(2,1)S(1)} fusion(s32[]{:T(128)S(6)} %select_n.92, bf16[2,4,4,128,1024]{4,3,0,2,1:T(8,128)(2,1)} %constant_dynamic-slice_fusion), kind=kLoop, calls=%fused_computation.43 | loop fusion | flops 4194304 | bytes 16777220 | tf_op jit(solution)/shard_map/jit(_roll_dynamic)/concatenate | solution.py:54
  431.5 3.8 fusion.59
  435.4 3.2 fusion.26
  438.8 8.5 %fusion.47 = f32[1024,1024]{1,0:T(8,128)} fusion(bf16[2048,1024]{1,0:T(8,128)(2,1)} %bitcast.148, bf16[1024,2048]{1,0:T(8,128)(2,1)S(1)} %copy-done.4, f32[2048]{0:T(1024)S(1)} %convert_element_type.102, f32[1024]{0:T(1024)S(1)} %add_rsqrt_fusion), kind=kOutput, calls=%fused_computation.78 | convolution fusion | flops 4303355904 | bytes 12595200 | tf_op jit(solution)/shard_map/dot_general | solution.py:139
  447.3 15.3 %convolution_convert_fusion.1 = bf16[1024,2048]{1,0:T(8,128)(2,1)} fusion(bf16[1024,2048]{0,1:T(8,128)(2,1)} %bitcast.144, f32[1024,1024]{1,0:T(8,128)} %fusion.47, bf16[2048,1024]{1,0:T(8,128)(2,1)} %bitcast.147, bf16[1024,2048]{1,0:T(8,128)(2,1)} %all-gather.5.cloned.1.call-done, f32[2048]{0:T(1024)S(1)} %convert_element_type.102, f32[1024]{0:T(1024)S(1)} %add_rsqrt_fusion), kind=kOutput, calls=%fused_computation.56 | convolution fusion | flops 8606711808 | bytes 20983808 | tf_op jit(solution)/shard_map/dot_general | solution.py:148
  466.0 37.6 %reduce-scatter.5.cloned.1.call-done = bf16[1024,256]{1,0:T(8,128)(2,1)} async-done(((bf16[1024,2048]{1,0:T(8,128)(2,1)}), bf16[1024,256]{1,0:T(8,128)(2,1)}) %reduce-scatter.5.cloned.1.call-update) | async-done | bytes 524304 | tf_op jit(solution)/shard_map/reduce_scatter | solution.py:151
  503.6 2.0 add_convert_fusion
  (126 shorter events, 33.1 us)
Async XLA Ops:
  7.2 17.5 %copy-start.13 = (bf16[1,4096,256]{2,1,0:T(8,128)(2,1)S(1)}, bf16[1,4096,256]{2,1,0:T(8,128)(2,1)}, u32[]{:S(2)}) copy-start(bf16[1,4096,256]{2,1,0:T(8,128)(2,1)} %param.22) | copy-start | bytes 6291460
  7.2 148.4 %all-gather.3.cloned.1.call-start = ((), (), s32[]{:S(2)}) async-start(), calls=%async_computation.2 | async-start | bytes 4718592 | tf_op jit(solution)/shard_map/all_gather | solution.py:89
  10.2 36.0 %collective-permute-start.8 = (bf16[1280,128]{0,1:T(8,128)(2,1)}, bf16[1280,128]{0,1:T(8,128)(2,1)S(1)}, u32[]{:S(2)}, u32[]{:S(2)}) collective-permute-start(bf16[1280,128]{0,1:T(8,128)(2,1)} %get-tuple-element.93), channel_id=1, source_target_pairs={{0,8},{8,16},{16,24},{24,0},{32,40},{40,48},{48,56},{56,32},{64,72... | collective-permute-start | bytes 983048 | tf_op jit(solution)/shard_map/ppermute | solution.py:50
  12.2 35.1 %collective-permute-start.7 = (bf16[1280,128]{0,1:T(8,128)(2,1)}, bf16[1280,128]{0,1:T(8,128)(2,1)S(1)}, u32[]{:S(2)}, u32[]{:S(2)}) collective-permute-start(bf16[1280,128]{0,1:T(8,128)(2,1)} %get-tuple-element.93), channel_id=1, source_target_pairs={{0,16},{8,24},{16,0},{24,8},{32,48},{40,56},{48,32},{56,40},{64,80... | collective-permute-start | bytes 983048 | tf_op jit(solution)/shard_map/ppermute | solution.py:50
  15.8 17.7 %collective-permute-start.2 = (bf16[3,128,256]{2,1,0:T(8,128)(2,1)}, bf16[3,128,256]{2,1,0:T(8,128)(2,1)S(1)}, u32[]{:S(2)}, u32[]{:S(2)}) collective-permute-start(bf16[3,128,256]{2,1,0:T(8,128)(2,1)} %param.14), channel_id=1, source_target_pairs={{0,8},{8,16},{16,24},{24,0},{32,40},{40,48},{48,56},{56,32},{64,72... | collective-permute-start | bytes 589832 | tf_op jit(solution)/shard_map/ppermute | solution.py:50
  15.8 23.2 %collective-permute-start.1 = (bf16[3,128,256]{2,1,0:T(8,128)(2,1)}, bf16[3,128,256]{2,1,0:T(8,128)(2,1)}, u32[]{:S(2)}, u32[]{:S(2)}) collective-permute-start(bf16[3,128,256]{2,1,0:T(8,128)(2,1)} %param.14), channel_id=1, source_target_pairs={{0,16},{8,24},{16,0},{24,8},{32,48},{40,56},{48,32},{56,40},{64,80... | collective-permute-start | bytes 589832 | tf_op jit(solution)/shard_map/ppermute | solution.py:50
  18.2 20.8 %collective-permute-start = (bf16[3,128,256]{2,1,0:T(8,128)(2,1)}, bf16[3,128,256]{2,1,0:T(8,128)(2,1)}, u32[]{:S(2)}, u32[]{:S(2)}) collective-permute-start(bf16[3,128,256]{2,1,0:T(8,128)(2,1)} %param.14), channel_id=1, source_target_pairs={{0,24},{8,0},{16,8},{24,16},{32,56},{40,32},{48,40},{56,48},{64,88... | collective-permute-start | bytes 589832 | tf_op jit(solution)/shard_map/ppermute | solution.py:50
  19.0 269.1 %reduce-scatter.3.cloned.1.call-start = ((), (), s32[]{:S(2)}) async-start(), calls=%async_computation.3 | async-start | bytes 4718592 | tf_op jit(solution)/shard_map/reduce_scatter | solution.py:132
  20.5 18.5 %copy-start.14 = (bf16[3,128,256]{2,1,0:T(8,128)(2,1)S(1)}, bf16[3,128,256]{2,1,0:T(8,128)(2,1)}, u32[]{:S(2)}) copy-start(bf16[3,128,256]{2,1,0:T(8,128)(2,1)} %param.14) | copy-start | bytes 589828
  33.4 13.8 %collective-permute-start.6 = (bf16[1280,128]{0,1:T(8,128)(2,1)}, bf16[1280,128]{0,1:T(8,128)(2,1)S(1)}, u32[]{:S(2)}, u32[]{:S(2)}) collective-permute-start(bf16[1280,128]{0,1:T(8,128)(2,1)} %get-tuple-element.93), channel_id=1, source_target_pairs={{0,24},{8,0},{16,8},{24,16},{32,56},{40,32},{48,40},{56,48},{64,88... | collective-permute-start | bytes 983048 | tf_op jit(solution)/shard_map/ppermute | solution.py:50
  40.1 37.9 %collective-permute-start.3 = (bf16[3,4,128,256]{3,2,0,1:T(8,128)(2,1)S(1)}, bf16[3,4,128,256]{3,2,0,1:T(8,128)(2,1)S(1)}, u32[]{:S(2)}, u32[]{:S(2)}) collective-permute-start(bf16[3,4,128,256]{3,2,0,1:T(8,128)(2,1)S(1)} %pad_maximum_fusion.2), channel_id=1, source_target_pairs={{0,96},{8,104},{16,112},{24,120},{32,0},{40,8},{48,16},{56,24},{64... | collective-permute-start | bytes 2359304 | tf_op jit(solution)/shard_map/ppermute | solution.py:52
  44.5 33.6 %collective-permute-start.4 = (bf16[3,4,128,256]{3,2,0,1:T(8,128)(2,1)S(1)}, bf16[3,4,128,256]{3,2,0,1:T(8,128)(2,1)S(1)}, u32[]{:S(2)}, u32[]{:S(2)}) collective-permute-start(bf16[3,4,128,256]{3,2,0,1:T(8,128)(2,1)S(1)} %pad_maximum_fusion.2), channel_id=1, source_target_pairs={{0,64},{8,72},{16,80},{24,88},{32,96},{40,104},{48,112},{56,120},{... | collective-permute-start | bytes 2359304 | tf_op jit(solution)/shard_map/ppermute | solution.py:52
  46.2 32.0 %copy-start.6 = (bf16[1280,128]{0,1:T(8,128)(2,1)}, bf16[1280,128]{0,1:T(8,128)(2,1)S(1)}, u32[]{:S(2)}) copy-start(bf16[1280,128]{0,1:T(8,128)(2,1)S(1)} %collective-permute-done.8) | copy-start | bytes 983044
  46.2 37.2 %collective-permute-start.5 = (bf16[3,4,128,256]{3,2,0,1:T(8,128)(2,1)S(1)}, bf16[3,4,128,256]{3,2,0,1:T(8,128)(2,1)S(1)}, u32[]{:S(2)}, u32[]{:S(2)}) collective-permute-start(bf16[3,4,128,256]{3,2,0,1:T(8,128)(2,1)S(1)} %pad_maximum_fusion.2), channel_id=1, source_target_pairs={{0,32},{8,40},{16,48},{24,56},{32,64},{40,72},{48,80},{56,88},{64,... | collective-permute-start | bytes 2359304 | tf_op jit(solution)/shard_map/ppermute | solution.py:52
  47.2 31.0 %copy-start.8 = (bf16[1280,128]{0,1:T(8,128)(2,1)}, bf16[1280,128]{0,1:T(8,128)(2,1)S(1)}, u32[]{:S(2)}) copy-start(bf16[1280,128]{0,1:T(8,128)(2,1)S(1)} %collective-permute-done.7) | copy-start | bytes 983044
  47.3 31.0 %copy-start.10 = (bf16[1280,128]{0,1:T(8,128)(2,1)}, bf16[1280,128]{0,1:T(8,128)(2,1)S(1)}, u32[]{:S(2)}) copy-start(bf16[1280,128]{0,1:T(8,128)(2,1)S(1)} %collective-permute-done.6) | copy-start | bytes 983044
  48.5 83.8 %collective-permute-start.9 = (bf16[1280,4,128]{0,2,1:T(8,128)(2,1)}, bf16[1280,4,128]{0,2,1:T(8,128)(2,1)}, u32[]{:S(2)}, u32[]{:S(2)}) collective-permute-start(bf16[1280,4,128]{0,2,1:T(8,128)(2,1)} %pad_maximum_fusion.1), channel_id=1, source_target_pairs={{0,96},{8,104},{16,112},{24,120},{32,0},{40,8},{48,16},{56,24},{64... | collective-permute-start | bytes 3932168 | tf_op jit(solution)/shard_map/ppermute | solution.py:52
  50.8 84.0 %collective-permute-start.10 = (bf16[1280,4,128]{0,2,1:T(8,128)(2,1)}, bf16[1280,4,128]{0,2,1:T(8,128)(2,1)}, u32[]{:S(2)}, u32[]{:S(2)}) collective-permute-start(bf16[1280,4,128]{0,2,1:T(8,128)(2,1)} %pad_maximum_fusion.1), channel_id=1, source_target_pairs={{0,64},{8,72},{16,80},{24,88},{32,96},{40,104},{48,112},{56,120},{... | collective-permute-start | bytes 3932168 | tf_op jit(solution)/shard_map/ppermute | solution.py:52
  78.1 59.2 %collective-permute-start.11 = (bf16[1280,4,128]{0,2,1:T(8,128)(2,1)}, bf16[1280,4,128]{0,2,1:T(8,128)(2,1)}, u32[]{:S(2)}, u32[]{:S(2)}) collective-permute-start(bf16[1280,4,128]{0,2,1:T(8,128)(2,1)} %pad_maximum_fusion.1), channel_id=1, source_target_pairs={{0,32},{8,40},{16,48},{24,56},{32,64},{40,72},{48,80},{56,88},{64,... | collective-permute-start | bytes 3932168 | tf_op jit(solution)/shard_map/ppermute | solution.py:52
  96.8 42.9 %copy-start.7 = (bf16[1280,128]{0,1:T(8,128)(2,1)S(1)}, bf16[1280,128]{0,1:T(8,128)(2,1)}, u32[]{:S(2)}) copy-start(bf16[1280,128]{0,1:T(8,128)(2,1)} %copy-done.6) | copy-start | bytes 983044
  96.8 42.9 %copy-start.9 = (bf16[1280,128]{0,1:T(8,128)(2,1)S(1)}, bf16[1280,128]{0,1:T(8,128)(2,1)}, u32[]{:S(2)}) copy-start(bf16[1280,128]{0,1:T(8,128)(2,1)} %copy-done.8) | copy-start | bytes 983044
  96.8 42.9 %copy-start.11 = (bf16[1280,128]{0,1:T(8,128)(2,1)S(1)}, bf16[1280,128]{0,1:T(8,128)(2,1)}, u32[]{:S(2)}) copy-start(bf16[1280,128]{0,1:T(8,128)(2,1)} %copy-done.10) | copy-start | bytes 983044
  153.2 2.3 copy-start
  155.6 3.5 copy-start.3
  164.6 1.7 copy-start.5
  164.6 1.0 copy-start.15
  164.6 1.2 copy-start.16
  164.6 2.4 copy-start.2
  209.6 78.6 %copy-start.12 = (bf16[1024,256]{1,0:T(8,128)(2,1)S(1)}, bf16[1024,256]{1,0:T(8,128)(2,1)}, u32[]{:S(2)}) copy-start(bf16[1024,256]{1,0:T(8,128)(2,1)} %param.13) | copy-start | bytes 1572868
  209.6 80.7 %copy-start.17 = (bf16[128,1024]{1,0:T(8,128)(2,1)S(1)}, bf16[128,1024]{1,0:T(8,128)(2,1)}, u32[]{:S(2)}) copy-start(bf16[128,1024]{1,0:T(8,128)(2,1)} %param.19) | copy-start | bytes 786436
  209.6 80.7 %copy-start.18 = (bf16[128,1024]{1,0:T(8,128)(2,1)S(1)}, bf16[128,1024]{1,0:T(8,128)(2,1)}, u32[]{:S(2)}) copy-start(bf16[128,1024]{1,0:T(8,128)(2,1)} %param.18) | copy-start | bytes 786436
  209.6 110.1 %copy-start.19 = (bf16[2048]{0:T(1024)(128)(2,1)S(1)}, bf16[2048]{0:T(1024)(128)(2,1)}, u32[]{:S(2)}) copy-start(bf16[2048]{0:T(1024)(128)(2,1)} %param.17) | copy-start | bytes 12292
  209.6 225.7 %all-gather.5.cloned.1.call-start = ((), (), s32[]{:S(2)}) async-start(), calls=%async_computation.4 | async-start | bytes 4718592 | tf_op jit(solution)/shard_map/all_gather | solution.py:136
  288.1 33.1 %slice-start = ((s8[5242880]{0:T(1024)(128)(4,1)}), s8[1048576]{0:T(1024)(128)(4,1)S(1)}, s32[]{:S(2)}) async-start(s8[5242880]{0:T(1024)(128)(4,1)} %bitcast.129), calls=%async_computation.6 | async-start | bytes 2097152
  290.2 213.4 %reduce-scatter.5.cloned.1.call-start = ((), (), s32[]{:S(2)}) async-start(), calls=%async_computation.5 | async-start | bytes 4718592 | tf_op jit(solution)/shard_map/reduce_scatter | solution.py:151
  290.4 15.0 %collective-permute-start.14 = (bf16[2,128,1024]{2,1,0:T(8,128)(2,1)S(1)}, bf16[2,128,1024]{2,1,0:T(8,128)(2,1)S(1)}, u32[]{:S(2)}, u32[]{:S(2)}) collective-permute-start(bf16[2,128,1024]{2,1,0:T(8,128)(2,1)S(1)} %get-tuple-element.91), channel_id=1, source_target_pairs={{0,8},{8,16},{16,24},{24,0},{32,40},{40,48},{48,56},{56,32},{64,72... | collective-permute-start | bytes 1572872 | tf_op jit(solution)/shard_map/ppermute | solution.py:50
  292.0 22.8 %collective-permute-start.13 = (bf16[2,128,1024]{2,1,0:T(8,128)(2,1)S(1)}, bf16[2,128,1024]{2,1,0:T(8,128)(2,1)S(1)}, u32[]{:S(2)}, u32[]{:S(2)}) collective-permute-start(bf16[2,128,1024]{2,1,0:T(8,128)(2,1)S(1)} %get-tuple-element.91), channel_id=1, source_target_pairs={{0,16},{8,24},{16,0},{24,8},{32,48},{40,56},{48,32},{56,40},{64,80... | collective-permute-start | bytes 1572872 | tf_op jit(solution)/shard_map/ppermute | solution.py:50
  294.8 19.9 %collective-permute-start.12 = (bf16[2,128,1024]{2,1,0:T(8,128)(2,1)S(1)}, bf16[2,128,1024]{2,1,0:T(8,128)(2,1)S(1)}, u32[]{:S(2)}, u32[]{:S(2)}) collective-permute-start(bf16[2,128,1024]{2,1,0:T(8,128)(2,1)S(1)} %get-tuple-element.91), channel_id=1, source_target_pairs={{0,24},{8,0},{16,8},{24,16},{32,56},{40,32},{48,40},{56,48},{64,88... | collective-permute-start | bytes 1572872 | tf_op jit(solution)/shard_map/ppermute | solution.py:50
  314.8 6.4 %slice-start.1 = ((s8[5242880]{0:T(1024)(128)(4,1)}), s8[4194304]{0:T(1024)(128)(4,1)S(1)}, s32[]{:S(2)}) async-start(s8[5242880]{0:T(1024)(128)(4,1)} %bitcast.129), calls=%async_computation.7 | async-start | bytes 8388608
  315.1 91.3 %collective-permute-start.15 = (bf16[2,4,128,1024]{3,2,0,1:T(8,128)(2,1)S(1)}, bf16[2,4,128,1024]{3,2,0,1:T(8,128)(2,1)S(1)}, u32[]{:S(2)}, u32[]{:S(2)}) collective-permute-start(bf16[2,4,128,1024]{3,2,0,1:T(8,128)(2,1)S(1)} %pad_maximum_fusion), channel_id=1, source_target_pairs={{0,96},{8,104},{16,112},{24,120},{32,0},{40,8},{48,16},{56,24},{64... | collective-permute-start | bytes 6291464 | tf_op jit(solution)/shard_map/ppermute | solution.py:52
  317.8 90.0 %collective-permute-start.16 = (bf16[2,4,128,1024]{3,2,0,1:T(8,128)(2,1)S(1)}, bf16[2,4,128,1024]{3,2,0,1:T(8,128)(2,1)S(1)}, u32[]{:S(2)}, u32[]{:S(2)}) collective-permute-start(bf16[2,4,128,1024]{3,2,0,1:T(8,128)(2,1)S(1)} %pad_maximum_fusion), channel_id=1, source_target_pairs={{0,64},{8,72},{16,80},{24,88},{32,96},{40,104},{48,112},{56,120},{... | collective-permute-start | bytes 6291464 | tf_op jit(solution)/shard_map/ppermute | solution.py:52
  318.6 91.4 %collective-permute-start.17 = (bf16[2,4,128,1024]{3,2,0,1:T(8,128)(2,1)S(1)}, bf16[2,4,128,1024]{3,2,0,1:T(8,128)(2,1)S(1)}, u32[]{:S(2)}, u32[]{:S(2)}) collective-permute-start(bf16[2,4,128,1024]{3,2,0,1:T(8,128)(2,1)S(1)} %pad_maximum_fusion), channel_id=1, source_target_pairs={{0,32},{8,40},{16,48},{24,56},{32,64},{40,72},{48,80},{56,88},{64,... | collective-permute-start | bytes 6291464 | tf_op jit(solution)/shard_map/ppermute | solution.py:52
  435.4 3.4 copy-start.4
  462.6 41.0 %copy-start.1 = (bf16[1024,256]{1,0:T(8,128)(2,1)S(1)}, bf16[1024,256]{1,0:T(8,128)(2,1)}, u32[]{:S(2)}) copy-start(bf16[1024,256]{1,0:T(8,128)(2,1)} %add_convert_fusion.1) | copy-start | bytes 1572868
Sparse Core Ops, SparseCore 0:
  19.1 37.3 all-gather.2
  209.7 78.3 reduce-scatter.2
  290.4 34.8 all-gather.4
  462.8 40.7 reduce-scatter.4

commit v2 on v0

--- a/solution.py
+++ b/solution.py
@@ -30,6 +30,23 @@
     )
 
 
+def gather_packed(blocks, axes, axis_name):
+    count = lax.axis_size(axis_name)
+    joined = jnp.concatenate([block.reshape(-1) for block in blocks])
+    gathered = lax.all_gather(joined, axis_name, axis=0, tiled=False)
+    outs = []
+    offset = 0
+    for block, axis in zip(blocks, axes):
+        size = block.size
+        piece = gathered[:, offset:offset + size].reshape((count,) + block.shape)
+        piece = jnp.moveaxis(piece, 0, axis)
+        shape = list(block.shape)
+        shape[axis] *= count
+        outs.append(piece.reshape(shape))
+        offset += size
+    return outs
+
+
 def absorb(carry, queries, keys, values, valid):
     top, total, accum = carry
     scores = jnp.einsum("qhd,khd->hqk", queries, keys, preferred_element_type=jnp.float32) * HD ** (
@@ -50,6 +67,10 @@
     hidden_in, w_qkv, w_out, attn_gain, mlp_gain, w_gate, w_up, w_down, k_cache, v_cache, cache_len
 ):
     new_count = hidden_in.shape[0]
+    w_qkv_full = lax.all_gather(w_qkv, "req", axis=1, tiled=True)
+    w_gate_full, w_up_full, w_down_full, w_out_full = gather_packed(
+        [w_gate, w_up, w_down, w_out], [0, 0, 1, 1], "req"
+    )
     width = w_qkv.shape[2]
     heads_local = width // HD
     slots = k_cache.shape[1]
@@ -59,7 +80,7 @@
     projected = jnp.einsum(
         "nd,kdw->knw",
         columns,
-        lax.all_gather(w_qkv, "req", axis=1, tiled=True),
+        w_qkv_full,
         preferred_element_type=jnp.float32,
     )
     length = cache_len[0]
@@ -94,26 +115,25 @@
     top, total, accum = lax.fori_loop(0, count, step_block, carry)
     attn = (accum / total).transpose(1, 0, 2).reshape(new_count, width).astype(jnp.bfloat16)
     partial_value = jnp.dot(
-        attn, lax.all_gather(w_out, "req", axis=1, tiled=True), preferred_element_type=jnp.float32
+        attn, w_out_full, preferred_element_type=jnp.float32
     )
-    summed = lax.psum_scatter(
-        partial_value.astype(jnp.bfloat16), "mp", scatter_dimension=1, tiled=True
-    ).astype(jnp.float32)
-    mid_local = (hidden_in.astype(jnp.float32) + summed).astype(jnp.bfloat16)
-    mid_full = lax.all_gather(mid_local, "mp", axis=1, tiled=True)
+    summed = lax.psum(partial_value.astype(jnp.bfloat16), "mp").astype(jnp.float32)
+    mid_full = (full_rows.astype(jnp.float32) + summed).astype(jnp.bfloat16)
+    own = hidden_in.shape[1]
+    mid_local = lax.dynamic_slice_in_dim(mid_full, lax.axis_index("mp") * own, own, axis=1)
     normed2 = rms_scale(mid_full, mlp_gain)
     columns = normed2
     gate = jnp.dot(
         columns,
-        lax.all_gather(w_gate, "req", axis=0, tiled=True),
+        w_gate_full,
         preferred_element_type=jnp.float32,
     )
     upper = jnp.dot(
-        columns, lax.all_gather(w_up, "req", axis=0, tiled=True), preferred_element_type=jnp.float32
+        columns, w_up_full, preferred_element_type=jnp.float32
     )
     units = (jax.nn.silu(gate) * upper).astype(jnp.bfloat16)
     terms = jnp.dot(
-        units, lax.all_gather(w_down, "req", axis=1, tiled=True), preferred_element_type=jnp.float32
+        units, w_down_full, preferred_element_type=jnp.float32
     )
     reduced = lax.psum_scatter(
         terms.astype(jnp.bfloat16), "mp", scatter_dimension=1, tiled=True

time: 500 us -> 371 us (0.74)
  waiting for transfers between devices: 365 us -> 205 us
  local copies, waits for them, and re-layouts: 13.8 us -> 65.6 us
  matrix products: 68.6 us -> 54.6 us
    all_gather x6 -> x2, waiting for transfers between devices: 241 us -> 103 us  [the longest x1 53.4 us: on_device(): w_qkv_full = lax.all_gather(w_qkv, 'req', axis=1, tiled=True)]
    reduce_scatter x1 -> x0, waiting for transfers between devices: 60 us -> none  [on_device(): lax.psum_scatter(partial_value.astype(jnp.bfloat16), 'mp', scatter_dimens...]
    psum x0 -> x1, waiting for transfers between devices: none -> 41.7 us  [on_device(): lax.psum(partial_value.astype(jnp.bfloat16), 'mp').astype(jnp.float32)]
    all_gather x0 -> x1, local copies, waits for them, and re-layouts: none -> 17.1 us  [gather_packed(): gathered = lax.all_gather(joined, axis_name, axis=0, tiled=False)]
    another operation x0 -> x2, local copies, waits for them, and re-layouts: none -> 9.61 us  [gather_packed(): outs.append(piece.reshape(shape))]
    slice x0 -> x1, local copies, waits for them, and re-layouts: none -> 9.09 us  [gather_packed(): piece = gathered[:, offset:offset + size].reshape((count,) + block.shape)]
    unnamed x15 -> x24, local copies, waits for them, and re-layouts: 12.2 us -> 20.4 us
    transpose x0 -> x2, local copies, waits for them, and re-layouts: none -> 6.97 us  [gather_packed(): piece = jnp.moveaxis(piece, 0, axis)]
  transfers between devices with their start and end apart: 9 -> 5, of which waited for: 8 -> 5; matrix products, arithmetic and copies ran while one was open for 19% -> 26% of each run, Pallas kernels for 0% -> 0%
where the time goes in v2:
time: 371 us; the launch traced here: 370 us
  waiting for transfers between devices  205 us (55%)
  local copies, waits for them, and re-layouts  65.6 us (18%)
  matrix products  54.6 us (15%)
  other arithmetic  30.3 us (8%)
  between operations  14.7 us (4%)
    all_gather x1, waiting for transfers between devices, on_device(): w_qkv_full = lax.all_gather(w_qkv, 'req', axis=1, tiled=True)  53.4 us
    all_gather x1, waiting for transfers between devices, gather_packed(): gathered = lax.all_gather(joined, axis_name, axis=0, tiled=False)  49.2 us
    psum x1, waiting for transfers between devices, on_device(): lax.psum(partial_value.astype(jnp.bfloat16), 'mp').astype(jnp.float32)  41.7 us
    reduce_scatter x1, waiting for transfers between devices, on_device(): lax.psum_scatter(terms.astype(jnp.bfloat16), 'mp', scatter_dimension=1, t...  34.8 us
    all_gather x1, waiting for transfers between devices, on_device(): full_rows = lax.all_gather(hidden_in, 'mp', axis=1, tiled=True)  24.8 us
    unnamed x24, local copies, waits for them, and re-layouts  20.4 us
    all_gather x1, local copies, waits for them, and re-layouts, gather_packed(): gathered = lax.all_gather(joined, axis_name, axis=0, tiled=False)  17.1 us
    dot_general x1, matrix products, on_device(): terms = jnp.dot(units, w_down_full, preferred_element_type=jnp.float32)  15.3 us
  transfers between devices with their start and end apart: 5, of which 5 were waited for; matrix products, arithmetic and copies ran while one was open for 26% of the time, Pallas kernels for 0%

profile of v2, /device:TPU:0, one launch (start us, length us, event | category | flops | bytes accessed | tf_op | source)
XLA Modules:
  0.0 370.3 jit_solution(8494943149520512240)
XLA Ops:
  7.2 0.0 all-gather.5.cloned.1.call-start
  7.2 0.7 all-gather.5.cloned.1.call-update
  7.9 0.0 all-gather.7.cloned.1.call-start
  8.0 1.7 copy.38
  9.7 0.0 all-gather.7.cloned.1.call-update
  9.7 0.0 all-gather.9.cloned.1.call-start
  9.8 1.0 copy.48
  10.8 1.0 copy.49
  11.8 2.0 pad_maximum_fusion
  13.7 0.0 all-gather.9.cloned.1.call-update
  13.8 0.0 all-reduce.2.cloned.1.call-start
  14.5 2.9 copy.40
  17.4 4.1 %copy.41 = bf16[1,4096,256]{1,2,0:T(8,128)(2,1)} copy(bf16[1,4096,256]{2,1,0:T(8,128)(2,1)} %param.22) | data formatting | bytes 4194304 | tf_op args[9]
  21.6 1.3 iota_compare_fusion
  22.9 0.5 multiply_cosine_fusion
  23.4 24.8 %all-gather.5.cloned.1.call-done = bf16[1024,2048]{1,0:T(8,128)(2,1)} async-done(((bf16[1024,256]{1,0:T(8,128)(2,1)}), bf16[1024,2048]{1,0:T(8,128)(2,1)}) %all-gather.5.cloned.1.call-update) | async-done | bytes 4194320 | tf_op jit(solution)/shard_map/all_gather | solution.py:77
  48.2 3.1 fusion.26
  51.3 53.4 %all-gather.7.cloned.1.call-done = bf16[3,2048,256]{1,2,0:T(8,128)(2,1)} async-done(((bf16[3,128,256]{1,2,0:T(8,128)(2,1)}), bf16[3,2048,256]{1,2,0:T(8,128)(2,1)}) %all-gather.7.cloned.1.call-update) | async-done | bytes 3145744 | tf_op jit(solution)/shard_map/all_gather | solution.py:70
  104.7 6.6 %fusion.38 = f32[3,1024,256]{1,2,0:T(8,128)S(1)} fusion(bf16[3,2048,256]{1,2,0:T(8,128)(2,1)} %all-gather.7.cloned.1.call-done, bf16[1024,2048]{1,0:T(8,128)(2,1)} %all-gather.5.cloned.1.call-done, f32[2048]{0:T(1024)S(1)} %convert_element_type.84, f32[1024]{0:T(1024)S(1)} %add_rsqrt_fusion.1), kind=kOutput, calls=%fused_computation.52 | convolution fusion | flops 3229614080 | bytes 10498048 | tf_op jit(solution)/shard_map/nd,kdw->knw/dot_general | solution.py:80
  111.3 1.0 slice.66
  112.3 0.1 fusion.57
  112.4 0.2 subtract_convert_fusion
  112.6 0.2 multiply_subtract_fusion
  112.8 0.3 copy-done.3
  113.1 0.7 copy-done.1
  113.8 3.0 fusion.20
  116.8 4.2 %fusion.22 = f32[4,1024]{1,0:T(4,128)S(1)} fusion(f32[4,1024,1024]{1,2,0:T(8,128)S(1)} %get-tuple-element.105, f32[4,1024]{1,0:T(4,128)S(1)} %get-tuple-element.101, pred[1024,1024]{0,1:T(8,128)(4,1)S(1)} %copy-done.1), kind=kLoop, calls=%fused_computation.31 | loop fusion | flops 20967424 | bytes 17858560 | tf_op jit(solution)/shard_map/reduce_sum | solution.py:59
  121.1 6.0 %fusion.41 = f32[4,1024,64]{1,2,0:T(8,128)} fusion(bf16[1024,4,64]{0,2,1:T(8,128)(2,1)S(1)} %bitcast.104, f32[4,1024,1024]{1,2,0:T(8,128)S(1)} %get-tuple-element.105, f32[4,1024]{1,0:T(4,128)S(1)} %get-tuple-element.101, pred[1024,1024]{0,1:T(8,128)(4,1)S(1)} %copy-done.1, f32[4,1024]{1,0:T(4,128)S(1)} %get-tuple-element.99), kind=kOutput, calls=%fused_computation.53 | convolution fusion | flops 558104576 | bytes 19431424 | tf_op jit(solution)/shard_map/hqk,khd->hqd/dot_general | solution.py:60
  127.1 24.0 %while.14 = (s32[]{:T(128)}, f32[4,1024,1]{1,0,2:T(4,128)S(1)}, f32[4,1024,1]{1,0,2:T(4,128)S(1)}, f32[4,1024,64]{1,2,0:T(8,128)}, s32[]{:T(128)}, /*index=5*/s3...) while((s32[]{:T(128)}, f32[4,1024,1]{1,0,2:T(4,128)S(1)}, ...), condition=%wide.region_6.7_spmd, body=%wide.region_3.6_spmd.sunk | while | flops 564671488 | bytes 36965104 | solution.py:115
  127.1 0.7 add_compare_fusion.2
  127.7 1.6 bitcast_reduce_fusion.2
  129.4 3.1 fusion.77
  132.4 2.5 fusion.76
  135.1 0.7 add_compare_fusion.2
  135.7 1.6 bitcast_reduce_fusion.2
  137.4 3.1 fusion.77
  140.4 2.5 fusion.76
  143.1 0.7 add_compare_fusion.2
  143.7 1.6 bitcast_reduce_fusion.2
  145.4 3.1 fusion.77
  148.4 2.5 fusion.76
  151.0 1.3 divide_convert_fusion
  152.4 49.2 %all-gather.9.cloned.1.call-done = bf16[6815744]{0:T(1024)(128)(2,1)} async-done(((bf16[425984]{0:T(1024)(128)(2,1)}), bf16[6815744]{0:T(1024)(128)(2,1)}) %all-gather.9.cloned.1.call-update) | async-done | bytes 13631504 | tf_op jit(solution)/shard_map/all_gather | solution.py:36
  201.5 17.1 %reshape.187 = bf16[16,425984]{1,0:T(8,128)(2,1)} reshape(bf16[6815744]{0:T(1024)(128)(2,1)} %all-gather.9.cloned.1.call-done) | data formatting | bytes 27262976 | tf_op jit(solution)/shard_map/all_gather | solution.py:36
  218.6 1.3 slice_bitcast_fusion.1
  219.9 0.2 copy.50
  220.1 0.5 copy.42
  220.6 3.4 convolution_convert_fusion
  224.0 0.0 all-reduce.2.cloned.1.call-update
  224.0 0.3 reduce-scatter.2.cloned.1.call-start
  224.3 9.1 %fusion.56 = (bf16[16,131072]{1,0:T(8,128)(2,1)}, bf16[2,8,1024,128]{3,1,2,0:T(8,128)(2,1)}, bf16[16,131072]{1,0:T(8,128)(2,1)}) fusion(bf16[16,425984]{1,0:T(8,128)(2,1)} %reshape.187), kind=kLoop, calls=%fused_computation.81 | loop fusion | bytes 25165824 | tf_op jit(solution)/shard_map/slice | solution.py:41
  233.4 4.8 %reshape_reshape.6 = bf16[2048,1024]{1,0:T(8,128)(2,1)} reshape(bf16[16,131072]{1,0:T(8,128)(2,1)} %get-tuple-element.92) | data formatting | bytes 8388608 | tf_op jit(solution)/shard_map/reshape;reshape | solution.py:45
  238.2 5.1 %copy.51 = bf16[2,8,1024,128]{3,2,1,0:T(8,128)(2,1)} copy(bf16[2,8,1024,128]{3,1,2,0:T(8,128)(2,1)} %get-tuple-element.91) | data formatting | bytes 8388608
  243.3 6.4 %copy.43 = bf16[1024,16,128]{0,2,1:T(8,128)(2,1)} copy(bf16[1024,16,128]{2,0,1:T(8,128)(2,1)} %bitcast.89) | data formatting | bytes 8388608 | tf_op jit(solution)/shard_map/transpose | solution.py:42
  249.7 4.8 %reshape_reshape.7 = bf16[2048,1024]{1,0:T(8,128)(2,1)} reshape(bf16[16,131072]{1,0:T(8,128)(2,1)} %get-tuple-element.90) | data formatting | bytes 8388608 | tf_op jit(solution)/shard_map/reshape;reshape | solution.py:45
  254.5 41.7 %all-reduce.2.cloned.1.call-done = bf16[1024,2048]{1,0:T(8,128)(2,1)} async-done(((bf16[1024,2048]{1,0:T(8,128)(2,1)}), bf16[1024,2048]{1,0:T(8,128)(2,1)}) %all-reduce.2.cloned.1.call-update) | async-done | bytes 4194320 | tf_op jit(solution)/shard_map/psum | solution.py:120
  296.2 5.6 %fusion.23 = (f32[1024]{0:T(1024)S(1)}, bf16[1024,2048]{1,0:T(8,128)(2,1)S(1)}) fusion(bf16[1024,2048]{1,0:T(8,128)(2,1)} %all-reduce.2.cloned.1.call-done, bf16[1024,2048]{1,0:T(8,128)(2,1)} %all-gather.5.cloned.1.call-done), kind=kLoop, calls=%fused_computation.34 | loop fusion | flops 14679040 | bytes 12587008 | tf_op jit(solution)/shard_map/reduce_sum | solution.py:16
  301.9 6.3 %fusion.45 = f32[1024,1024]{1,0:T(8,128)} fusion(bf16[2048,1024]{1,0:T(8,128)(2,1)S(1)} %copy-done.2, bf16[1024,2048]{1,0:T(8,128)(2,1)S(1)} %get-tuple-element.87, f32[2048]{0:T(1024)S(1)} %convert_element_type.99, f32[1024]{0:T(1024)S(1)} %add_rsqrt_fusion), kind=kOutput, calls=%fused_computation.54 | convolution fusion | flops 4303355904 | bytes 12595200 | tf_op jit(solution)/shard_map/dot_general | solution.py:126
  308.2 15.3 %convolution_convert_fusion.1 = bf16[1024,2048]{1,0:T(8,128)(2,1)} fusion(bf16[1024,2048]{0,1:T(8,128)(2,1)} %bitcast.94, f32[1024,1024]{1,0:T(8,128)} %fusion.45, bf16[2048,1024]{1,0:T(8,128)(2,1)} %reshape_reshape.7, bf16[1024,2048]{1,0:T(8,128)(2,1)} %copy-done, f32[2048]{0:T(1024)S(1)} %convert_element_type.99, f32[1024]{0:T(1024)S(1)} %add_rsqrt_fusion), kind=kOutput, calls=%fused_computation.51 | convolution fusion | flops 8606711808 | bytes 20983808 | tf_op jit(solution)/shard_map/dot_general | solution.py:135
  323.6 1.0 copy.44
  324.6 1.3 slice_bitcast_fusion.2
  325.9 1.0 copy.45
  326.9 34.8 %reduce-scatter.2.cloned.1.call-done = bf16[1024,256]{1,0:T(8,128)(2,1)} async-done(((bf16[1024,2048]{1,0:T(8,128)(2,1)}), bf16[1024,256]{1,0:T(8,128)(2,1)}) %reduce-scatter.2.cloned.1.call-update) | async-done | bytes 524304 | tf_op jit(solution)/shard_map/reduce_scatter | solution.py:138
  361.7 2.1 add_convert_fusion
  (44 shorter events, 0.3 us)
Async XLA Ops:
  7.2 7.3 %copy-start.7 = (bf16[2048]{0:T(1024)(128)(2,1)S(1)}, bf16[2048]{0:T(1024)(128)(2,1)}, u32[]{:S(2)}) copy-start(bf16[2048]{0:T(1024)(128)(2,1)} %param.16) | copy-start | bytes 12292
  7.2 41.0 %all-gather.5.cloned.1.call-start = ((), (), s32[]{:S(2)}) async-start(), calls=%async_computation.1 | async-start | bytes 4718592 | tf_op jit(solution)/shard_map/all_gather | solution.py:77
  7.9 96.8 %all-gather.7.cloned.1.call-start = ((), (), s32[]{:S(2)}) async-start(), calls=%async_computation.2 | async-start | bytes 3342336 | tf_op jit(solution)/shard_map/all_gather | solution.py:70
  9.7 191.8 %all-gather.9.cloned.1.call-start = ((), (), s32[]{:S(2)}) async-start(), calls=%async_computation.5 | async-start | bytes 14483456 | tf_op jit(solution)/shard_map/all_gather | solution.py:36
  13.8 282.5 %all-reduce.2.cloned.1.call-start = ((), (), s32[]{:S(2)}) async-start(), calls=%async_computation.3 | async-start | bytes 8388608 | tf_op jit(solution)/shard_map/psum | solution.py:120
  14.5 7.0 %copy-start.8 = (bf16[2048]{0:T(1024)(128)(2,1)S(1)}, bf16[2048]{0:T(1024)(128)(2,1)}, u32[]{:S(2)}) copy-start(bf16[2048]{0:T(1024)(128)(2,1)} %param.17) | copy-start | bytes 12292
  111.3 1.8 copy-start.3
  112.3 1.5 copy-start.1
  116.8 4.2 %copy-start.6 = (bf16[1,1024,256]{1,2,0:T(8,128)(2,1)S(1)}, bf16[1,1024,256]{1,2,0:T(8,128)(2,1)}, u32[]{:S(2)}) copy-start(bf16[1,1024,256]{1,2,0:T(8,128)(2,1)} %slice.66) | copy-start | bytes 1572868
  127.7 1.6 copy-start.4
  132.4 2.6 copy-start.5
  135.7 1.6 copy-start.4
  140.4 2.6 copy-start.5
  143.7 1.6 copy-start.4
  148.4 2.6 copy-start.5
  224.0 137.7 %reduce-scatter.2.cloned.1.call-start = ((), (), s32[]{:S(2)}) async-start(), calls=%async_computation.4 | async-start | bytes 4718592 | tf_op jit(solution)/shard_map/reduce_scatter | solution.py:138
  296.2 5.6 %copy-start.2 = (bf16[2048,1024]{1,0:T(8,128)(2,1)S(1)}, bf16[2048,1024]{1,0:T(8,128)(2,1)}, u32[]{:S(2)}) copy-start(bf16[2048,1024]{1,0:T(8,128)(2,1)} %reshape_reshape.6) | copy-start | bytes 12582916
  301.9 6.3 %copy-start = (bf16[1024,2048]{1,0:T(8,128)(2,1)}, bf16[1024,2048]{1,0:T(8,128)(2,1)S(1)}, u32[]{:S(2)}) copy-start(bf16[1024,2048]{1,0:T(8,128)(2,1)S(1)} %get-tuple-element.87) | copy-start | bytes 12582916
Sparse Core Ops, SparseCore 0:
  9.7 38.4 all-gather.4
  50.9 53.7 all-gather.6
  106.9 94.6 all-gather.8
  224.1 72.0 all-reduce.1
  323.7 37.9 reduce-scatter.1

commit v3 on v2

--- a/solution.py
+++ b/solution.py
@@ -32,18 +32,19 @@
 
 def gather_packed(blocks, axes, axis_name):
     count = lax.axis_size(axis_name)
-    joined = jnp.concatenate([block.reshape(-1) for block in blocks])
+    lane = 128
+    joined = jnp.concatenate([block.reshape(-1, lane) for block in blocks], axis=0)
     gathered = lax.all_gather(joined, axis_name, axis=0, tiled=False)
     outs = []
     offset = 0
     for block, axis in zip(blocks, axes):
-        size = block.size
-        piece = gathered[:, offset:offset + size].reshape((count,) + block.shape)
+        rows = block.size // lane
+        piece = gathered[:, offset:offset + rows].reshape((count,) + block.shape)
         piece = jnp.moveaxis(piece, 0, axis)
         shape = list(block.shape)
         shape[axis] *= count
         outs.append(piece.reshape(shape))
-        offset += size
+        offset += rows
     return outs
 
 

time: 371 us -> 355 us (0.957)
  waiting for transfers between devices: 205 us -> 164 us
  matrix products: 54.6 us -> 77.8 us
  local copies, waits for them, and re-layouts: 65.6 us -> 49 us
  other arithmetic: 30.3 us -> 46.5 us
    all_gather x1, waiting for transfers between devices: 49.2 us -> 9.18 us  [gather_packed(): gathered = lax.all_gather(joined, axis_name, axis=0, tiled=False)]
    all_gather x1 -> x0, local copies, waits for them, and re-layouts: 17.1 us -> none  [gather_packed(): gathered = lax.all_gather(joined, axis_name, axis=0, tiled=False)]
    dot_general x4 -> x9, matrix products: 15.2 us -> 30.5 us  [absorb(): jnp.einsum('hqk,khd->hqd', probs.astype(jnp.bfloat16), values, preferred_...]
    reduce_sum x4 -> x9, other arithmetic: 11.8 us -> 24.6 us  [absorb(): total = total * factor + jnp.sum(probs, axis=-1, keepdims=True)]
    unnamed x24 -> x19, local copies, waits for them, and re-layouts: 20.4 us -> 12.2 us
    dot_general x4 -> x9, matrix products: 7.79 us -> 15.7 us  [absorb(): jnp.einsum('qhd,khd->hqk', queries, keys, preferred_element_type=jnp.floa...]
    another operation x2, local copies, waits for them, and re-layouts: 9.61 us -> 14.8 us  [gather_packed(): outs.append(piece.reshape(shape))]
    transpose x2 -> x3, local copies, waits for them, and re-layouts: 6.97 us -> 8.26 us  [gather_packed(): piece = jnp.moveaxis(piece, 0, axis)]
  transfers between devices with their start and end apart: 5 -> 5, of which waited for: 5 -> 5; matrix products, arithmetic and copies ran while one was open for 26% -> 39% of each run, Pallas kernels for 0% -> 0%
where the time goes in v3:
time: 355 us; the launch traced here: 353 us
  waiting for transfers between devices  164 us (46%)
  matrix products  77.8 us (22%)
  local copies, waits for them, and re-layouts  49 us (14%)
  other arithmetic  46.5 us (13%)
  between operations  14.7 us (4%)
    all_gather x1, waiting for transfers between devices, on_device(): w_qkv_full = lax.all_gather(w_qkv, 'req', axis=1, tiled=True)  53.4 us
    psum x1, waiting for transfers between devices, on_device(): lax.psum(partial_value.astype(jnp.bfloat16), 'mp').astype(jnp.float32)  41.3 us
    reduce_scatter x1, waiting for transfers between devices, on_device(): lax.psum_scatter(terms.astype(jnp.bfloat16), 'mp', scatter_dimension=1, t...  34.8 us
    dot_general x9, matrix products, absorb(): jnp.einsum('hqk,khd->hqd', probs.astype(jnp.bfloat16), values, preferred_...  30.5 us
    all_gather x1, waiting for transfers between devices, on_device(): full_rows = lax.all_gather(hidden_in, 'mp', axis=1, tiled=True)  24.7 us
    reduce_sum x9, other arithmetic, absorb(): total = total * factor + jnp.sum(probs, axis=-1, keepdims=True)  24.6 us
    dot_general x9, matrix products, absorb(): jnp.einsum('qhd,khd->hqk', queries, keys, preferred_element_type=jnp.floa...  15.7 us
    dot_general x1, matrix products, on_device(): terms = jnp.dot(units, w_down_full, preferred_element_type=jnp.float32)  15.4 us
  transfers between devices with their start and end apart: 5, of which 5 were waited for; matrix products, arithmetic and copies ran while one was open for 39% of the time, Pallas kernels for 0%

profile of v3, /device:TPU:0, one launch (start us, length us, event | category | flops | bytes accessed | tf_op | source)
XLA Modules:
  0.0 353.2 jit_solution(15132475671423839923)
XLA Ops:
  7.2 0.7 all-gather.5.cloned.1.call-update
  8.0 1.7 copy.29
  9.8 1.1 reshape.167
  10.8 1.1 reshape.168
  11.9 2.0 pad_maximum_fusion
  14.6 2.9 copy.31
  17.6 4.1 %copy.32 = bf16[1,4096,256]{1,2,0:T(8,128)(2,1)} copy(bf16[1,4096,256]{2,1,0:T(8,128)(2,1)} %param.22) | data formatting | bytes 4194304 | tf_op args[9]
  21.7 1.3 iota_compare_fusion
  23.5 24.7 %all-gather.5.cloned.1.call-done = bf16[1024,2048]{1,0:T(8,128)(2,1)} async-done(((bf16[1024,256]{1,0:T(8,128)(2,1)}), bf16[1024,2048]{1,0:T(8,128)(2,1)}) %all-gather.5.cloned.1.call-update) | async-done | bytes 4194320 | tf_op jit(solution)/shard_map/all_gather | solution.py:78
  48.2 3.1 fusion.26
  51.3 53.4 %all-gather.7.cloned.1.call-done = bf16[3,2048,256]{1,2,0:T(8,128)(2,1)} async-done(((bf16[3,128,256]{1,2,0:T(8,128)(2,1)}), bf16[3,2048,256]{1,2,0:T(8,128)(2,1)}) %all-gather.7.cloned.1.call-update) | async-done | bytes 3145744 | tf_op jit(solution)/shard_map/all_gather | solution.py:71
  104.7 6.6 %fusion.38 = f32[3,1024,256]{1,2,0:T(8,128)S(1)} fusion(bf16[3,2048,256]{1,2,0:T(8,128)(2,1)} %all-gather.7.cloned.1.call-done, bf16[1024,2048]{1,0:T(8,128)(2,1)} %all-gather.5.cloned.1.call-done, f32[2048]{0:T(1024)S(1)} %convert_element_type.84, f32[1024]{0:T(1024)S(1)} %add_rsqrt_fusion.1), kind=kOutput, calls=%fused_computation.52 | convolution fusion | flops 3229614080 | bytes 10498048 | tf_op jit(solution)/shard_map/nd,kdw->knw/dot_general | solution.py:81
  111.3 1.0 slice.66
  113.1 0.7 copy-done.1
  113.8 3.0 fusion.20
  116.8 4.2 %fusion.22 = f32[4,1024]{1,0:T(4,128)S(1)} fusion(f32[4,1024,1024]{1,2,0:T(8,128)S(1)} %get-tuple-element.102, f32[4,1024]{1,0:T(4,128)S(1)} %get-tuple-element.98, pred[1024,1024]{0,1:T(8,128)(4,1)S(1)} %copy-done.1), kind=kLoop, calls=%fused_computation.31 | loop fusion | flops 20967424 | bytes 17858560 | tf_op jit(solution)/shard_map/reduce_sum | solution.py:60
  121.1 5.9 %fusion.41 = f32[4,1024,64]{1,2,0:T(8,128)} fusion(bf16[1024,4,64]{0,2,1:T(8,128)(2,1)S(1)} %bitcast.91, f32[4,1024,1024]{1,2,0:T(8,128)S(1)} %get-tuple-element.102, f32[4,1024]{1,0:T(4,128)S(1)} %get-tuple-element.98, pred[1024,1024]{0,1:T(8,128)(4,1)S(1)} %copy-done.1, f32[4,1024]{1,0:T(4,128)S(1)} %get-tuple-element.96), kind=kOutput, calls=%fused_computation.53 | convolution fusion | flops 558104576 | bytes 19431424 | tf_op jit(solution)/shard_map/hqk,khd->hqd/dot_general | solution.py:61
  127.0 64.0 %while.14 = (s32[]{:T(128)}, f32[4,1024,1]{1,0,2:T(4,128)S(1)}, f32[4,1024,1]{1,0,2:T(4,128)S(1)}, f32[4,1024,64]{1,2,0:T(8,128)}, s32[]{:T(128)}, /*index=5*/s3...) while((s32[]{:T(128)}, f32[4,1024,1]{1,0,2:T(4,128)S(1)}, ...), condition=%wide.region_6.7_spmd, body=%wide.region_3.6_spmd.sunk | while | flops 564671488 | bytes 36965104 | solution.py:116
  127.7 1.6 bitcast_reduce_fusion.2
  129.3 3.1 fusion.77
  132.4 2.5 fusion.76
  135.0 0.7 add_compare_fusion.2
  135.7 1.6 bitcast_reduce_fusion.2
  137.3 3.1 fusion.77
  140.4 2.5 fusion.76
  143.0 0.7 add_compare_fusion.2
  143.7 1.6 bitcast_reduce_fusion.2
  145.3 3.1 fusion.77
  148.4 2.5 fusion.76
  151.0 0.7 add_compare_fusion.2
  151.7 1.6 bitcast_reduce_fusion.2
  153.3 3.1 fusion.77
  156.4 2.5 fusion.76
  159.7 1.6 bitcast_reduce_fusion.2
  161.3 3.1 fusion.77
  164.4 2.5 fusion.76
  167.0 0.7 add_compare_fusion.2
  167.7 1.6 bitcast_reduce_fusion.2
  169.3 3.1 fusion.77
  172.4 2.5 fusion.76
  175.0 0.7 add_compare_fusion.2
  175.7 1.6 bitcast_reduce_fusion.2
  177.3 3.1 fusion.77
  180.4 2.5 fusion.76
  183.7 1.6 bitcast_reduce_fusion.2
  185.3 3.1 fusion.77
  188.4 2.5 fusion.76
  191.0 1.3 divide_convert_fusion
  192.4 9.2 %all-gather.9.cloned.1.call-done = bf16[53248,128]{1,0:T(8,128)(2,1)} async-done(((bf16[3328,128]{1,0:T(8,128)(2,1)}), bf16[53248,128]{1,0:T(8,128)(2,1)}) %all-gather.9.cloned.1.call-update) | async-done | bytes 13631504 | tf_op jit(solution)/shard_map/all_gather | solution.py:37
  201.5 1.3 slice_bitcast_fusion.1
  203.4 3.3 convolution_convert_fusion
  207.4 9.1 %fusion.56 = (bf16[16,1024,128]{2,1,0:T(8,128)(2,1)}, bf16[1024,16,128]{2,0,1:T(8,128)(2,1)}, bf16[16,1024,128]{2,1,0:T(8,128)(2,1)}) fusion(bf16[16,3328,128]{2,1,0:T(8,128)(2,1)} %bitcast.79), kind=kLoop, calls=%fused_computation.81 | loop fusion | bytes 25165824 | tf_op jit(solution)/shard_map/slice | solution.py:42
  216.5 7.4 %reshape_reshape.6 = bf16[2048,1024]{1,0:T(8,128)(2,1)} reshape(bf16[16,1024,128]{2,1,0:T(8,128)(2,1)} %get-tuple-element.89) | data formatting | bytes 8388608 | tf_op jit(solution)/shard_map/reshape;reshape | solution.py:46
  223.9 6.4 %copy.34 = bf16[1024,16,128]{0,2,1:T(8,128)(2,1)} copy(bf16[1024,16,128]{2,0,1:T(8,128)(2,1)} %get-tuple-element.88) | data formatting | bytes 8388608 | tf_op jit(solution)/shard_map/transpose | solution.py:43
  230.4 7.4 %reshape_reshape.7 = bf16[2048,1024]{1,0:T(8,128)(2,1)} reshape(bf16[16,1024,128]{2,1,0:T(8,128)(2,1)} %get-tuple-element.87) | data formatting | bytes 8388608 | tf_op jit(solution)/shard_map/reshape;reshape | solution.py:46
  237.8 41.3 %all-reduce.2.cloned.1.call-done = bf16[1024,2048]{1,0:T(8,128)(2,1)} async-done(((bf16[1024,2048]{1,0:T(8,128)(2,1)}), bf16[1024,2048]{1,0:T(8,128)(2,1)}) %all-reduce.2.cloned.1.call-update) | async-done | bytes 4194320 | tf_op jit(solution)/shard_map/psum | solution.py:121
  279.1 5.6 %fusion.23 = (f32[1024]{0:T(1024)S(1)}, bf16[1024,2048]{1,0:T(8,128)(2,1)S(1)}) fusion(bf16[1024,2048]{1,0:T(8,128)(2,1)} %all-reduce.2.cloned.1.call-done, bf16[1024,2048]{1,0:T(8,128)(2,1)} %all-gather.5.cloned.1.call-done), kind=kLoop, calls=%fused_computation.34 | loop fusion | flops 14679040 | bytes 12587008 | tf_op jit(solution)/shard_map/reduce_sum | solution.py:16
  284.7 6.3 %fusion.45 = f32[1024,1024]{1,0:T(8,128)} fusion(bf16[2048,1024]{1,0:T(8,128)(2,1)S(1)} %copy-done.2, bf16[1024,2048]{1,0:T(8,128)(2,1)S(1)} %get-tuple-element.84, f32[2048]{0:T(1024)S(1)} %convert_element_type.99, f32[1024]{0:T(1024)S(1)} %add_rsqrt_fusion), kind=kOutput, calls=%fused_computation.54 | convolution fusion | flops 4303355904 | bytes 12595200 | tf_op jit(solution)/shard_map/dot_general | solution.py:127
  291.0 15.4 %convolution_convert_fusion.1 = bf16[1024,2048]{1,0:T(8,128)(2,1)} fusion(bf16[1024,2048]{0,1:T(8,128)(2,1)} %bitcast.84, f32[1024,1024]{1,0:T(8,128)} %fusion.45, bf16[2048,1024]{1,0:T(8,128)(2,1)} %reshape_reshape.7, bf16[1024,2048]{1,0:T(8,128)(2,1)} %copy-done, f32[2048]{0:T(1024)S(1)} %convert_element_type.99, f32[1024]{0:T(1024)S(1)} %add_rsqrt_fusion), kind=kOutput, calls=%fused_computation.51 | convolution fusion | flops 8606711808 | bytes 20983808 | tf_op jit(solution)/shard_map/dot_general | solution.py:136
  306.5 1.0 copy.35
  307.5 1.3 slice_bitcast_fusion.2
  308.8 1.0 copy.36
  309.8 34.8 %reduce-scatter.2.cloned.1.call-done = bf16[1024,256]{1,0:T(8,128)(2,1)} async-done(((bf16[1024,2048]{1,0:T(8,128)(2,1)}), bf16[1024,256]{1,0:T(8,128)(2,1)}) %reduce-scatter.2.cloned.1.call-update) | async-done | bytes 524304 | tf_op jit(solution)/shard_map/reduce_scatter | solution.py:139
  344.5 2.1 add_convert_fusion
  (96 shorter events, 5.3 us)
Async XLA Ops:
  7.2 7.4 %copy-start.7 = (bf16[2048]{0:T(1024)(128)(2,1)S(1)}, bf16[2048]{0:T(1024)(128)(2,1)}, u32[]{:S(2)}) copy-start(bf16[2048]{0:T(1024)(128)(2,1)} %param.16) | copy-start | bytes 12292
  7.2 41.0 %all-gather.5.cloned.1.call-start = ((), (), s32[]{:S(2)}) async-start(), calls=%async_computation.1 | async-start | bytes 4718592 | tf_op jit(solution)/shard_map/all_gather | solution.py:78
  7.9 96.8 %all-gather.7.cloned.1.call-start = ((), (), s32[]{:S(2)}) async-start(), calls=%async_computation.2 | async-start | bytes 3342336 | tf_op jit(solution)/shard_map/all_gather | solution.py:71
  9.7 191.8 %all-gather.9.cloned.1.call-start = ((), (), s32[]{:S(2)}) async-start(), calls=%async_computation.5 | async-start | bytes 14483456 | tf_op jit(solution)/shard_map/all_gather | solution.py:37
  13.9 265.2 %all-reduce.2.cloned.1.call-start = ((), (), s32[]{:S(2)}) async-start(), calls=%async_computation.3 | async-start | bytes 8388608 | tf_op jit(solution)/shard_map/psum | solution.py:121
  111.3 1.8 copy-start.3
  112.3 1.5 copy-start.1
  116.8 4.2 %copy-start.6 = (bf16[1,1024,256]{1,2,0:T(8,128)(2,1)S(1)}, bf16[1,1024,256]{1,2,0:T(8,128)(2,1)}, u32[]{:S(2)}) copy-start(bf16[1,1024,256]{1,2,0:T(8,128)(2,1)} %slice.66) | copy-start | bytes 1572868
  127.7 1.6 copy-start.4
  132.4 2.6 copy-start.5
  135.7 1.6 copy-start.4
  140.4 2.6 copy-start.5
  143.7 1.6 copy-start.4
  148.4 2.6 copy-start.5
  151.7 1.6 copy-start.4
  156.4 2.6 copy-start.5
  159.7 1.6 copy-start.4
  164.4 2.6 copy-start.5
  167.7 1.6 copy-start.4
  172.4 2.6 copy-start.5
  175.7 1.6 copy-start.4
  180.4 2.6 copy-start.5
  183.7 1.6 copy-start.4
  188.4 2.6 copy-start.5
  206.7 0.7 copy-start.8
  206.7 137.8 %reduce-scatter.2.cloned.1.call-start = ((), (), s32[]{:S(2)}) async-start(), calls=%async_computation.4 | async-start | bytes 4718592 | tf_op jit(solution)/shard_map/reduce_scatter | solution.py:139
  279.1 5.6 %copy-start.2 = (bf16[2048,1024]{1,0:T(8,128)(2,1)S(1)}, bf16[2048,1024]{1,0:T(8,128)(2,1)}, u32[]{:S(2)}) copy-start(bf16[2048,1024]{1,0:T(8,128)(2,1)} %reshape_reshape.6) | copy-start | bytes 12582916
  284.7 6.4 %copy-start = (bf16[1024,2048]{1,0:T(8,128)(2,1)}, bf16[1024,2048]{1,0:T(8,128)(2,1)S(1)}, u32[]{:S(2)}) copy-start(bf16[1024,2048]{1,0:T(8,128)(2,1)S(1)} %get-tuple-element.84) | copy-start | bytes 12582916
Sparse Core Ops, SparseCore 0:
  9.7 38.4 all-gather.4
  50.9 53.7 all-gather.6
  106.9 94.6 all-gather.8
  206.9 72.1 all-reduce.1
  306.5 37.9 reduce-scatter.1

commit v4 on v3

--- a/solution.py
+++ b/solution.py
@@ -2,6 +2,9 @@
 import jax.numpy as jnp
 from jax import lax
 from jax.sharding import PartitionSpec as P
+from jax.experimental import pallas as pl
+from jax.experimental.pallas import tpu as pltpu
+import functools
 
 HD = 64
 
@@ -48,20 +51,94 @@
     return outs
 
 
-def absorb(carry, queries, keys, values, valid):
-    top, total, accum = carry
-    scores = jnp.einsum("qhd,khd->hqk", queries, keys, preferred_element_type=jnp.float32) * HD ** (
-        -0.5
-    )
-    scores = jnp.where(valid[None], scores, NEG_FILL)
-    new_top = jnp.maximum(top, jnp.max(scores, axis=-1, keepdims=True))
-    factor = jnp.exp(top - new_top)
-    probs = jnp.where(valid[None], jnp.exp(scores - new_top), 0.0)
-    total = total * factor + jnp.sum(probs, axis=-1, keepdims=True)
-    accum = accum * factor + jnp.einsum(
-        "hqk,khd->hqd", probs.astype(jnp.bfloat16), values, preferred_element_type=jnp.float32
-    )
-    return (new_top, total, accum)
+def flash_body(len_ref, q_ref, kc_ref, vc_ref, kn_ref, vn_ref, o_ref, m_sc, l_sc, acc_sc, *, tk, n_cache, scale):
+    j = pl.program_id(1)
+    length = len_ref[0]
+    tq = q_ref.shape[1]
+
+    @pl.when(j == 0)
+    def _():
+        m_sc[...] = jnp.full(m_sc.shape, NEG_FILL, jnp.float32)
+        l_sc[...] = jnp.zeros(l_sc.shape, jnp.float32)
+        acc_sc[...] = jnp.zeros(acc_sc.shape, jnp.float32)
+
+    def update(k, v, mask):
+        s = lax.dot_general(q_ref[0], k, (((1,), (1,)), ((), ())), preferred_element_type=jnp.float32) * scale
+        if mask is not None:
+            s = jnp.where(mask, s, NEG_FILL)
+        m_prev = m_sc[...]
+        m_new = jnp.maximum(m_prev, jnp.max(s, axis=1, keepdims=True))
+        alpha = jnp.exp(m_prev - m_new)
+        p = jnp.exp(s - m_new)
+        if mask is not None:
+            p = jnp.where(mask, p, 0.0)
+        l_sc[...] = alpha * l_sc[...] + jnp.sum(p, axis=1, keepdims=True)
+        acc_sc[...] = alpha * acc_sc[...] + jnp.dot(p.astype(jnp.bfloat16), v, preferred_element_type=jnp.float32)
+        m_sc[...] = m_new
+
+    begin = j * tk
+
+    @pl.when((j < n_cache) & (begin + tk <= length))
+    def _():
+        update(kc_ref[0], vc_ref[0], None)
+
+    @pl.when((j < n_cache) & (begin < length) & (begin + tk > length))
+    def _():
+        col = begin + lax.broadcasted_iota(jnp.int32, (tq, tk), 1)
+        update(kc_ref[0], vc_ref[0], col < length)
+
+    @pl.when(j == n_cache)
+    def _():
+        row = lax.broadcasted_iota(jnp.int32, (tq, tq), 0)
+        col = lax.broadcasted_iota(jnp.int32, (tq, tq), 1)
+        update(kn_ref[0], vn_ref[0], row >= col)
+        o_ref[0] = (acc_sc[...] / l_sc[...]).astype(o_ref.dtype)
+
+
+def flash_attention(length, q, kc, vc, kn, vn):
+    heads, new_count, hd = q.shape
+    slots = kc.shape[1]
+    tk = min(new_count, slots)
+    n_cache = slots // tk
+    body = functools.partial(flash_body, tk=tk, n_cache=n_cache, scale=hd ** (-0.5))
+
+    def cache_map(h, j, len_ref):
+        last = jnp.maximum(len_ref[0] - 1, 0) // tk
+        return (h, jnp.minimum(j, last), 0)
+
+    fixed = lambda h, j, len_ref: (h, 0, 0)
+    grid_spec = pltpu.PrefetchScalarGridSpec(
+        num_scalar_prefetch=1,
+        grid=(heads, n_cache + 1),
+        in_specs=[
+            pl.BlockSpec((1, new_count, hd), fixed),
+            pl.BlockSpec((1, tk, hd), cache_map),
+            pl.BlockSpec((1, tk, hd), cache_map),
+            pl.BlockSpec((1, new_count, hd), fixed),
+            pl.BlockSpec((1, new_count, hd), fixed),
+        ],
+        out_specs=pl.BlockSpec((1, new_count, hd), fixed),
+        scratch_shapes=[
+            pltpu.VMEM((new_count, 1), jnp.float32),
+            pltpu.VMEM((new_count, 1), jnp.float32),
+            pltpu.VMEM((new_count, hd), jnp.float32),
+        ],
+    )
+    flops = 4 * heads * new_count * (slots + new_count) * hd
+    cost = pl.CostEstimate(
+        flops=flops,
+        transcendentals=heads * new_count * (slots + new_count),
+        bytes_accessed=2 * (q.size + kc.size + vc.size + kn.size + vn.size) + 4 * q.size,
+    )
+    return pl.pallas_call(
+        body,
+        grid_spec=grid_spec,
+        out_shape=jax.ShapeDtypeStruct((heads, new_count, hd), jnp.bfloat16),
+        compiler_params=pltpu.CompilerParams(
+            dimension_semantics=("arbitrary", "arbitrary"), vmem_limit_bytes=56 * 1024 * 1024
+        ),
+        cost_estimate=cost,
+    )(length, q, kc, vc, kn, vn)
 
 
 def on_device(
@@ -93,28 +170,16 @@
         jnp.bfloat16
     )
     fresh_values = projected[2].astype(jnp.bfloat16).reshape(new_count, heads_local, HD)
-    rows = jnp.arange(new_count, dtype=jnp.int32)
-    causal = rows[:, None] >= rows[None, :]
-    start_carry = (
-        jnp.full((heads_local, new_count, 1), NEG_FILL, jnp.float32),
-        jnp.zeros((heads_local, new_count, 1), jnp.float32),
-        jnp.zeros((heads_local, new_count, HD), jnp.float32),
-    )
-    carry = absorb(start_carry, queries, fresh_keys, fresh_values, causal)
-    cache_keys = k_cache[0].reshape(slots, heads_local, HD)
-    cache_values = v_cache[0].reshape(slots, heads_local, HD)
-    block = min(slots, 512)
-    count = (length + block - 1) // block
-
-    def step_block(index, state):
-        begin = index * block
-        keys = lax.dynamic_slice_in_dim(cache_keys, begin, block, 0)
-        values = lax.dynamic_slice_in_dim(cache_values, begin, block, 0)
-        valid = (begin + jnp.arange(block, dtype=jnp.int32) < length)[None, :]
-        return absorb(state, queries, keys, values, valid)
-
-    top, total, accum = lax.fori_loop(0, count, step_block, carry)
-    attn = (accum / total).transpose(1, 0, 2).reshape(new_count, width).astype(jnp.bfloat16)
+    head_major = lambda array: array.reshape(array.shape[0], heads_local, HD).transpose(1, 0, 2)
+    attn_heads = flash_attention(
+        cache_len,
+        queries.transpose(1, 0, 2),
+        head_major(k_cache[0]),
+        head_major(v_cache[0]),
+        fresh_keys.transpose(1, 0, 2),
+        fresh_values.transpose(1, 0, 2),
+    )
+    attn = attn_heads.transpose(1, 0, 2).reshape(new_count, width)
     partial_value = jnp.dot(
         attn, w_out_full, preferred_element_type=jnp.float32
     )

time: 355 us -> 357 us (level)
  Pallas kernels: 0 us -> 58.5 us
  matrix products: 77.8 us -> 32.7 us
  other arithmetic: 46.5 us -> 21.8 us
  local copies, waits for them, and re-layouts: 49 us -> 72.4 us
  waiting for transfers between devices: 164 us -> 156 us
    pallas_call x0 -> x1, Pallas kernels: none -> 58.5 us  [flash_attention(): pl.pallas_call(body, grid_spec=grid_spec, out_shape=jax.ShapeDtypeStruct(...]
    dot_general x18 -> x0, matrix products: 46.2 us -> none  [the longest x9 30.5 us: absorb(): jnp.einsum('hqk,khd->hqd', probs.astype(jnp.bfloat16), values, preferred_...]
    reduce_sum x9 -> x0, other arithmetic: 24.6 us -> none  [absorb(): total = total * factor + jnp.sum(probs, axis=-1, keepdims=True)]
    unnamed x19 -> x25, local copies, waits for them, and re-layouts: 12.2 us -> 21.3 us
    another operation x0 -> x2, local copies, waits for them, and re-layouts: none -> 6.42 us  [on_device(): array.reshape(array.shape[0], heads_local, HD).transpose(1, 0, 2)]
    all_gather x1, waiting for transfers between devices: 24.7 us -> 19.2 us  [on_device(): full_rows = lax.all_gather(hidden_in, 'mp', axis=1, tiled=True)]
    lt x8 -> x0, other arithmetic: 5.24 us -> none  [step_block(): valid = (begin + jnp.arange(block, dtype=jnp.int32) < length)[None, :]]
  transfers between devices with their start and end apart: 5 -> 5, of which waited for: 5 -> 5; matrix products, arithmetic and copies ran while one was open for 39% -> 25% of each run, Pallas kernels for 0% -> 16%
where the time goes in v4:
time: 357 us; the launch traced here: 356 us
  waiting for transfers between devices  156 us (44%)
  local copies, waits for them, and re-layouts  72.4 us (20%)
  Pallas kernels  58.5 us (16%)
  matrix products  32.7 us (9%)
  other arithmetic  21.8 us (6%)
  between operations  14.6 us (4%)
    pallas_call x1, Pallas kernels, flash_attention(): pl.pallas_call(body, grid_spec=grid_spec, out_shape=jax.ShapeDtypeStruct(...  58.5 us
    all_gather x1, waiting for transfers between devices, on_device(): w_qkv_full = lax.all_gather(w_qkv, 'req', axis=1, tiled=True)  53.4 us
    psum x1, waiting for transfers between devices, on_device(): lax.psum(partial_value.astype(jnp.bfloat16), 'mp').astype(jnp.float32)  41.4 us
    reduce_scatter x1, waiting for transfers between devices, on_device(): lax.psum_scatter(terms.astype(jnp.bfloat16), 'mp', scatter_dimension=1, t...  33.9 us
    unnamed x25, local copies, waits for them, and re-layouts  21.3 us
    all_gather x1, waiting for transfers between devices, on_device(): full_rows = lax.all_gather(hidden_in, 'mp', axis=1, tiled=True)  19.2 us
    dot_general x1, matrix products, on_device(): terms = jnp.dot(units, w_down_full, preferred_element_type=jnp.float32)  15.4 us
    another operation x2, local copies, waits for them, and re-layouts, gather_packed(): outs.append(piece.reshape(shape))  14.7 us
  transfers between devices with their start and end apart: 5, of which 5 were waited for; matrix products, arithmetic and copies ran while one was open for 25% of the time, Pallas kernels for 16%

profile of v4, /device:TPU:0, one launch (start us, length us, event | category | flops | bytes accessed | tf_op | source)
XLA Modules:
  0.0 356.1 jit_solution(9460480216239655915)
XLA Ops:
  7.2 0.0 copy-start.6
  7.2 0.0 all-gather.5.cloned.1.call-start
  7.2 0.7 all-gather.5.cloned.1.call-update
  7.9 0.0 all-gather.7.cloned.1.call-start
  8.0 1.7 copy.30
  9.7 0.0 all-gather.7.cloned.1.call-update
  9.7 0.0 all-gather.9.cloned.1.call-start
  9.8 1.1 reshape.116
  10.8 1.1 reshape.117
  11.9 1.9 pad_maximum_fusion
  13.9 0.0 all-gather.9.cloned.1.call-update
  13.9 0.0 all-reduce.2.cloned.1.call-start
  13.9 0.0 copy-done.6
  14.6 2.9 copy.33
  17.5 3.2 copy.34
  20.7 3.1 copy.35
  23.9 3.2 copy.36
  27.1 1.9 multiply_cosine_fusion
  29.0 19.2 %all-gather.5.cloned.1.call-done = bf16[1024,2048]{1,0:T(8,128)(2,1)} async-done(((bf16[1024,256]{1,0:T(8,128)(2,1)}), bf16[1024,2048]{1,0:T(8,128)(2,1)}) %all-gather.5.cloned.1.call-update) | async-done | bytes 4194320 | tf_op jit(solution)/shard_map/all_gather | solution.py:155
  48.2 3.1 fusion.3
  51.3 53.4 %all-gather.7.cloned.1.call-done = bf16[3,2048,256]{1,2,0:T(8,128)(2,1)} async-done(((bf16[3,128,256]{1,2,0:T(8,128)(2,1)}), bf16[3,2048,256]{1,2,0:T(8,128)(2,1)}) %all-gather.7.cloned.1.call-update) | async-done | bytes 3145744 | tf_op jit(solution)/shard_map/all_gather | solution.py:148
  104.7 6.6 %fusion.12 = f32[3,1024,256]{1,2,0:T(8,128)S(1)} fusion(bf16[3,2048,256]{1,2,0:T(8,128)(2,1)} %all-gather.7.cloned.1.call-done, bf16[1024,2048]{1,0:T(8,128)(2,1)} %all-gather.5.cloned.1.call-done, f32[2048]{0:T(1024)S(1)} %convert_element_type.69, f32[1024]{0:T(1024)S(1)} %add_rsqrt_fusion.1), kind=kOutput, calls=%fused_computation.25 | convolution fusion | flops 3229614080 | bytes 10498048 | tf_op jit(solution)/shard_map/nd,kdw->knw/dot_general | solution.py:158
  111.3 0.0 copy-start.4
  111.3 0.9 slice.58
  112.3 0.2 fusion.23
  112.5 1.1 fusion.24
  113.6 0.0 copy-done.4
  113.6 3.0 copy.48
  116.6 3.0 copy.49
  119.6 0.9 fusion.25
  120.5 3.0 copy.46
  123.5 1.9 copy.47
  125.4 0.0 copy-done.5
  125.4 1.3 copy.39
  126.7 2.9 multiply_subtract_fusion
  129.7 1.6 fusion.32.kn_ref
  131.2 0.0 copy-done
  131.2 0.5 subtract_convert_fusion
  131.8 1.6 maximum_bitcast_fusion.q_ref
  133.3 58.5 %shard_map.130 = bf16[4,1024,64]{2,1,0:T(8,128)(2,1)} custom-call(s32[1]{0:T(128)} %copy.51.len_ref, bf16[4,1024,64]{2,1,0:T(8,128)(2,1)} %maximum_bitcast_fusion.q_ref, bf16[4,4096,64]{2,1,0:T(8,128)(2,1)} %bitcast.44, bf16[4,4096,64]{2,1,0:T(8,128)(2,1)} %bitcast.45, bf16[4,1024,64]{2,1,0:T(8,128)(2,1)} %fusion.32.kn_ref, bf16[4,1024,64]{2,1,0:T(8,128)(2,1)} %bitcast.52), custom_call_target="tpu_custom_call" | custom-call | flops 5368709120 | bytes 6815744 | tf_op jit(solution)/shard_map/pallas_call | solution.py:133
  191.9 2.3 copy.40
  194.2 7.3 %all-gather.9.cloned.1.call-done = bf16[53248,128]{1,0:T(8,128)(2,1)} async-done(((bf16[3328,128]{1,0:T(8,128)(2,1)}), bf16[53248,128]{1,0:T(8,128)(2,1)}) %all-gather.9.cloned.1.call-update) | async-done | bytes 13631504 | tf_op jit(solution)/shard_map/all_gather | solution.py:40
  201.5 2.3 slice_bitcast_fusion.1
  203.8 1.5 copy.41
  205.3 4.3 %convolution_convert_fusion = bf16[1024,2048]{1,0:T(8,128)(2,1)} fusion(bf16[1024,256]{0,1:T(8,128)(2,1)} %bitcast.49, bf16[256,2048]{0,1:T(8,128)(2,1)S(1)} %bitcast.43), kind=kOutput, calls=%fused_computation.18 | convolution fusion | flops 1075838976 | bytes 5767168 | tf_op jit(solution)/shard_map/dot_general | solution.py:183
  209.6 0.0 all-reduce.2.cloned.1.call-update
  209.7 0.0 reduce-scatter.2.cloned.1.call-start
  209.7 0.6 copy-done.7
  210.3 9.1 %fusion.22 = (bf16[16,1024,128]{2,1,0:T(8,128)(2,1)}, bf16[1024,16,128]{2,0,1:T(8,128)(2,1)}, bf16[16,1024,128]{2,1,0:T(8,128)(2,1)}) fusion(bf16[16,3328,128]{2,1,0:T(8,128)(2,1)} %bitcast.40), kind=kLoop, calls=%fused_computation.39 | loop fusion | bytes 25165824 | tf_op jit(solution)/shard_map/slice | solution.py:45
  219.5 7.4 %reshape_reshape.6 = bf16[2048,1024]{1,0:T(8,128)(2,1)} reshape(bf16[16,1024,128]{2,1,0:T(8,128)(2,1)} %get-tuple-element.16) | data formatting | bytes 8388608 | tf_op jit(solution)/shard_map/reshape;reshape | solution.py:49
  226.8 6.4 %copy.42 = bf16[1024,16,128]{0,2,1:T(8,128)(2,1)} copy(bf16[1024,16,128]{2,0,1:T(8,128)(2,1)} %get-tuple-element.15) | data formatting | bytes 8388608 | tf_op jit(solution)/shard_map/transpose | solution.py:46
  233.2 7.4 %reshape_reshape.7 = bf16[2048,1024]{1,0:T(8,128)(2,1)} reshape(bf16[16,1024,128]{2,1,0:T(8,128)(2,1)} %get-tuple-element.14) | data formatting | bytes 8388608 | tf_op jit(solution)/shard_map/reshape;reshape | solution.py:49
  240.6 41.4 %all-reduce.2.cloned.1.call-done = bf16[1024,2048]{1,0:T(8,128)(2,1)} async-done(((bf16[1024,2048]{1,0:T(8,128)(2,1)}), bf16[1024,2048]{1,0:T(8,128)(2,1)}) %all-reduce.2.cloned.1.call-update) | async-done | bytes 4194320 | tf_op jit(solution)/shard_map/psum | solution.py:186
  282.0 5.6 %fusion = (f32[1024]{0:T(1024)S(1)}, bf16[1024,2048]{1,0:T(8,128)(2,1)S(1)}) fusion(bf16[1024,2048]{1,0:T(8,128)(2,1)} %all-reduce.2.cloned.1.call-done, bf16[1024,2048]{1,0:T(8,128)(2,1)} %all-gather.5.cloned.1.call-done), kind=kLoop, calls=%fused_computation.5 | loop fusion | flops 14679040 | bytes 12587008 | tf_op jit(solution)/shard_map/reduce_sum | solution.py:19
  287.6 6.3 %fusion.16 = f32[1024,1024]{1,0:T(8,128)} fusion(bf16[2048,1024]{1,0:T(8,128)(2,1)S(1)} %copy-done.3, bf16[1024,2048]{1,0:T(8,128)(2,1)S(1)} %get-tuple-element.13, f32[2048]{0:T(1024)S(1)} %convert_element_type.80, f32[1024]{0:T(1024)S(1)} %add_rsqrt_fusion), kind=kOutput, calls=%fused_computation.26 | convolution fusion | flops 4303355904 | bytes 12595200 | tf_op jit(solution)/shard_map/dot_general | solution.py:192
  293.9 15.4 %convolution_convert_fusion.1 = bf16[1024,2048]{1,0:T(8,128)(2,1)} fusion(bf16[1024,2048]{0,1:T(8,128)(2,1)} %bitcast.46, f32[1024,1024]{1,0:T(8,128)} %fusion.16, bf16[2048,1024]{1,0:T(8,128)(2,1)} %reshape_reshape.7, bf16[1024,2048]{1,0:T(8,128)(2,1)} %copy-done.2, f32[2048]{0:T(1024)S(1)} %convert_element_type.80, f32[1024]{0:T(1024)S(1)} %add_rsqrt_fusion), kind=kOutput, calls=%fused_computation.19 | convolution fusion | flops 8606711808 | bytes 20983808 | tf_op jit(solution)/shard_map/dot_general | solution.py:201
  309.4 0.0 reduce-scatter.2.cloned.1.call-update
  309.4 0.6 maximum_convert_fusion
  310.0 0.3 copy.43
  310.3 1.0 copy.44
  311.3 1.3 slice_bitcast_fusion.2
  312.6 1.0 copy.45
  313.6 33.9 %reduce-scatter.2.cloned.1.call-done = bf16[1024,256]{1,0:T(8,128)(2,1)} async-done(((bf16[1024,2048]{1,0:T(8,128)(2,1)}), bf16[1024,256]{1,0:T(8,128)(2,1)}) %reduce-scatter.2.cloned.1.call-update) | async-done | bytes 524304 | tf_op jit(solution)/shard_map/reduce_scatter | solution.py:204
  347.5 2.1 add_convert_fusion.1
  (15 shorter events, 0.1 us)
Async XLA Ops:
  7.2 6.8 %copy-start.6 = (bf16[2048]{0:T(1024)(128)(2,1)S(1)}, bf16[2048]{0:T(1024)(128)(2,1)}, u32[]{:S(2)}) copy-start(bf16[2048]{0:T(1024)(128)(2,1)} %param.14) | copy-start | bytes 12292
  7.2 41.0 %all-gather.5.cloned.1.call-start = ((), (), s32[]{:S(2)}) async-start(), calls=%async_computation.1 | async-start | bytes 4718592 | tf_op jit(solution)/shard_map/all_gather | solution.py:155
  7.9 96.8 %all-gather.7.cloned.1.call-start = ((), (), s32[]{:S(2)}) async-start(), calls=%async_computation.2 | async-start | bytes 3342336 | tf_op jit(solution)/shard_map/all_gather | solution.py:148
  9.7 191.8 %all-gather.9.cloned.1.call-start = ((), (), s32[]{:S(2)}) async-start(), calls=%async_computation.5 | async-start | bytes 14483456 | tf_op jit(solution)/shard_map/all_gather | solution.py:40
  13.9 268.1 %all-reduce.2.cloned.1.call-start = ((), (), s32[]{:S(2)}) async-start(), calls=%async_computation.3 | async-start | bytes 8388608 | tf_op jit(solution)/shard_map/psum | solution.py:186
  111.3 2.3 copy-start.4
  119.6 5.8 %copy-start.5 = (bf16[1,1024,256]{1,2,0:T(8,128)(2,1)S(1)}, bf16[1,1024,256]{1,2,0:T(8,128)(2,1)}, u32[]{:S(2)}) copy-start(bf16[1,1024,256]{1,2,0:T(8,128)(2,1)} %slice.58) | copy-start | bytes 1572868
  126.7 4.5 %copy-start = (f32[1024,4,32]{2,0,1:T(8,128)S(1)}, f32[1024,4,32]{2,0,1:T(8,128)}, u32[]{:S(2)}) copy-start(f32[1024,4,32]{2,0,1:T(8,128)} %copy.46) | copy-start | bytes 1572868
  126.7 4.5 %copy-start.1 = (f32[1024,4,32]{2,0,1:T(8,128)S(1)}, f32[1024,4,32]{2,0,1:T(8,128)}, u32[]{:S(2)}) copy-start(f32[1024,4,32]{2,0,1:T(8,128)} %copy.47) | copy-start | bytes 1572868
  209.6 0.7 copy-start.7
  209.7 137.8 %reduce-scatter.2.cloned.1.call-start = ((), (), s32[]{:S(2)}) async-start(), calls=%async_computation.4 | async-start | bytes 4718592 | tf_op jit(solution)/shard_map/reduce_scatter | solution.py:204
  281.9 5.6 %copy-start.3 = (bf16[2048,1024]{1,0:T(8,128)(2,1)S(1)}, bf16[2048,1024]{1,0:T(8,128)(2,1)}, u32[]{:S(2)}) copy-start(bf16[2048,1024]{1,0:T(8,128)(2,1)} %reshape_reshape.6) | copy-start | bytes 12582916
  287.6 6.4 %copy-start.2 = (bf16[1024,2048]{1,0:T(8,128)(2,1)}, bf16[1024,2048]{1,0:T(8,128)(2,1)S(1)}, u32[]{:S(2)}) copy-start(bf16[1024,2048]{1,0:T(8,128)(2,1)S(1)} %get-tuple-element.13) | copy-start | bytes 12582916
Sparse Core Ops, SparseCore 0:
  9.7 38.4 all-gather.4
  50.9 53.7 all-gather.6
  106.9 94.6 all-gather.8
  209.8 72.1 all-reduce.1
  309.5 37.9 reduce-scatter.1

commit v5 on v4

--- a/solution.py
+++ b/solution.py
@@ -31,6 +31,24 @@
     return jnp.concatenate(
         [first * cosine - second * sine, second * cosine + first * sine], axis=-1
     )
+
+
+def gather_req_shifted(block, axis, axis_name):
+    count = lax.axis_size(axis_name)
+    side = int(round(count ** 0.5))
+    me = lax.axis_index(axis_name)
+    row, col = me // side, me % side
+
+    def inner(k):
+        return [(s, (s // side) * side + (s % side - k) % side) for s in range(count)]
+
+    def outer(k):
+        return [(s, ((s // side - k) % side) * side + s % side) for s in range(count)]
+
+    parts = [block] + [lax.ppermute(block, axis_name, inner(k)) for k in range(1, side)]
+    stage = jnp.stack(parts, axis=axis)
+    parts = [stage] + [lax.ppermute(stage, axis_name, outer(k)) for k in range(1, side)]
+    return jnp.stack(parts, axis=axis), row, col
 
 
 def gather_packed(blocks, axes, axis_name):
@@ -145,7 +163,9 @@
     hidden_in, w_qkv, w_out, attn_gain, mlp_gain, w_gate, w_up, w_down, k_cache, v_cache, cache_len
 ):
     new_count = hidden_in.shape[0]
-    w_qkv_full = lax.all_gather(w_qkv, "req", axis=1, tiled=True)
+    qkv_shifted, row, col = gather_req_shifted(w_qkv, 1, "req")
+    side = qkv_shifted.shape[1]
+    w_qkv_full = qkv_shifted.reshape(3, -1, w_qkv.shape[2])
     w_gate_full, w_up_full, w_down_full, w_out_full = gather_packed(
         [w_gate, w_up, w_down, w_out], [0, 0, 1, 1], "req"
     )
@@ -154,7 +174,8 @@
     slots = k_cache.shape[1]
     full_rows = lax.all_gather(hidden_in, "mp", axis=1, tiled=True)
     normed = rms_scale(full_rows, attn_gain)
-    columns = normed
+    blocks = normed.reshape(new_count, side, side, -1)
+    columns = jnp.roll(blocks, (-row, -col), axis=(1, 2)).reshape(new_count, -1)
     projected = jnp.einsum(
         "nd,kdw->knw",
         columns,

time: 357 us -> 331 us (0.927); the launches traced: 356 us -> 325 us
  waiting for transfers between devices: 156 us -> 107 us
  local copies, waits for them, and re-layouts: 72.4 us -> 83.8 us
  starting transfers between devices: 0.2 us -> 10.4 us
  Pallas kernels: 58.5 us -> 48.4 us
  other arithmetic: 21.8 us -> 29.4 us
    all_gather x1 -> x0, waiting for transfers between devices: 53.4 us -> none  [on_device(): w_qkv_full = lax.all_gather(w_qkv, 'req', axis=1, tiled=True)]
    ppermute x0 -> x6, waiting for transfers between devices: none -> 10.8 us  [the longest x3 10.8 us: gather_req_shifted(): lax.ppermute(stage, axis_name, outer(k))]
    ppermute x0 -> x6, starting transfers between devices: none -> 10.3 us  [the longest x3 5.45 us: gather_req_shifted(): lax.ppermute(block, axis_name, inner(k))]
    psum x1, waiting for transfers between devices: 41.4 us -> 51.5 us  [on_device(): lax.psum(partial_value.astype(jnp.bfloat16), 'mp').astype(jnp.float32)]
    pallas_call x1, Pallas kernels: 58.5 us -> 48.4 us  [flash_attention(): pl.pallas_call(body, grid_spec=grid_spec, out_shape=jax.ShapeDtypeStruct(...]
    all_gather x1, waiting for transfers between devices: 19.2 us -> 9.52 us  [on_device(): full_rows = lax.all_gather(hidden_in, 'mp', axis=1, tiled=True)]
    all_gather x1, waiting for transfers between devices: 7.32 us -> 0.01 us  [gather_packed(): gathered = lax.all_gather(joined, axis_name, axis=0, tiled=False)]
    convert_element_type x0 -> x1, local copies, waits for them, and re-layouts: none -> 6.4 us  [rms_scale(): (values * lax.rsqrt(meansq + EPSILON) * gain.astype(jnp.float32)).astype(...]
  transfers between devices with their start and end apart: 5 -> 10, of which waited for: 5 -> 4; matrix products, arithmetic and copies ran while one was open for 25% -> 33% of each run, Pallas kernels for 16% -> 15%
where the time goes in v5:
time: 331 us; the launch traced here: 325 us
  waiting for transfers between devices  107 us (32%)
  local copies, waits for them, and re-layouts  83.8 us (25%)
  Pallas kernels  48.4 us (15%)
  matrix products  31.3 us (9%)
  other arithmetic  29.4 us (9%)
  between operations  15.1 us (5%)
  starting transfers between devices  10.4 us (3%)
    psum x1, waiting for transfers between devices, on_device(): lax.psum(partial_value.astype(jnp.bfloat16), 'mp').astype(jnp.float32)  51.5 us
    pallas_call x1, Pallas kernels, flash_attention(): pl.pallas_call(body, grid_spec=grid_spec, out_shape=jax.ShapeDtypeStruct(...  48.4 us
    reduce_scatter x1, waiting for transfers between devices, on_device(): lax.psum_scatter(terms.astype(jnp.bfloat16), 'mp', scatter_dimension=1, t...  33.9 us
    unnamed x29, local copies, waits for them, and re-layouts  19.9 us
    dot_general x1, matrix products, on_device(): terms = jnp.dot(units, w_down_full, preferred_element_type=jnp.float32)  15.4 us
    another operation x2, local copies, waits for them, and re-layouts, gather_packed(): outs.append(piece.reshape(shape))  14.6 us
    ppermute x3, waiting for transfers between devices, gather_req_shifted(): lax.ppermute(stage, axis_name, outer(k))  10.8 us
    transpose x3, local copies, waits for them, and re-layouts, gather_packed(): piece = jnp.moveaxis(piece, 0, axis)  10.4 us
  transfers between devices with their start and end apart: 10, of which 4 were waited for; matrix products, arithmetic and copies ran while one was open for 33% of the time, Pallas kernels for 15%

profile of v5, /device:TPU:0, one launch (start us, length us, event | category | flops | bytes accessed | tf_op | source)
XLA Modules:
  0.0 325.0 jit_solution(10709362238983002610)
XLA Ops:
  7.2 0.0 all-gather.4.cloned.1.call-start
  7.2 0.7 all-gather.4.cloned.1.call-update
  7.9 0.0 all-gather.6.cloned.1.call-start
  8.0 1.1 reshape.122
  9.0 1.1 reshape.123
  10.1 2.0 pad_maximum_fusion
  12.1 0.0 all-gather.6.cloned.1.call-update
  12.1 0.0 all-reduce.2.cloned.1.call-start
  12.1 0.2 copy.45
  12.3 4.2 %collective-permute-start = (bf16[3,128,256]{1,2,0:T(8,128)(2,1)S(1)}, bf16[3,128,256]{1,2,0:T(8,128)(2,1)S(1)}, u32[]{:S(2)}, u32[]{:S(2)}) collective-permute-start(bf16[3,128,256]{1,2,0:T(8,128)(2,1)S(1)} %copy.45), channel_id=1, source_target_pairs={{0,24},{8,0},{16,8},{24,16},{32,56},{40,32},{48,40},{56,48},{64,88... | collective-permute-start | bytes 589832 | tf_op jit(solution)/shard_map/ppermute | solution.py:48
  16.5 1.3 collective-permute-start.2
  18.4 3.0 copy.54
  21.4 3.2 copy.55
  24.6 2.9 copy.56
  27.5 3.2 copy.57
  30.8 1.9 multiply_cosine_fusion
  32.7 1.2 fusion.32
  33.9 3.1 collective-permute-start.3
  37.0 0.6 collective-permute-start.4
  37.6 1.1 collective-permute-start.5
  38.7 9.5 %all-gather.4.cloned.1.call-done = bf16[1024,2048]{1,0:T(8,128)(2,1)} async-done(((bf16[1024,256]{1,0:T(8,128)(2,1)}), bf16[1024,2048]{1,0:T(8,128)(2,1)}) %all-gather.4.cloned.1.call-update) | async-done | bytes 4194320 | tf_op jit(solution)/shard_map/all_gather | solution.py:175
  48.2 3.2 fusion.3
  51.5 0.2 copy-done
  51.7 3.1 fusion.5
  54.8 6.4 %copy.49 = bf16[1024,2048]{0,1:T(8,128)(2,1)} copy(bf16[1024,2048]{1,0:T(8,128)(2,1)} %fusion.5) | data formatting | bytes 8388608 | tf_op jit(solution)/shard_map/convert_element_type | solution.py:20
  61.2 6.3 %copy.50 = bf16[1024,4,4,128]{3,0,2,1:T(8,128)(2,1)} copy(bf16[1024,4,4,128]{0,3,2,1:T(8,128)(2,1)} %bitcast.54) | data formatting | bytes 8388608 | tf_op jit(solution)/shard_map/reshape | solution.py:177
  67.5 3.1 fusion.11
  70.7 10.8 %collective-permute-done.5 = bf16[3,4,128,256]{2,3,1,0:T(8,128)(2,1)} collective-permute-done((bf16[3,4,128,256]{2,3,1,0:T(8,128)(2,1)S(1)}, bf16[3,4,128,256]{2,3,1,0:T(8,128)(2,1)}, u32[]{:S(2)}, u32[]{:S(2)}) %collective-permute-start.5) | collective-permute-done | bytes 786464 | tf_op jit(solution)/shard_map/ppermute | solution.py:50
  81.5 5.2 %fusion.19 = f32[3,1024,256]{1,2,0:T(8,128)S(1)} fusion(s32[]{:T(128)S(6)} %select_n.41, bf16[1024,4,4,128]{3,0,2,1:T(8,128)(2,1)S(1)} %fusion.11, bf16[3,1,4,128,256]{3,4,2,0,1:T(8,128)(2,1)} %bitcast.7, bf16[3,1,4,128,256]{3,4,2,0,1:T(8,128)(2,1)} %bitcast.6, bf16[3,1,4,128,256]{3,4,2,0,1:T(8,128)(2,1)} %bitcast.5, ...), kind=kOutput, calls=%fused_computation.36 | convolution fusion | flops 3228041216 | bytes 10485764 | tf_op jit(solution)/shard_map/nd,kdw->knw/dot_general | solution.py:179
  86.7 1.0 slice.58
  87.6 0.1 fusion.35
  87.8 1.1 fusion.36
  88.8 3.0 copy.71
  91.8 3.0 copy.72
  94.8 0.9 fusion.37
  95.7 3.1 copy.69
  98.8 1.9 copy.70
  100.7 1.3 copy.60
  102.1 3.0 multiply_subtract_fusion
  105.0 1.6 fusion.43.kn_ref
  106.6 0.5 subtract_convert_fusion
  107.1 1.6 maximum_bitcast_fusion.q_ref
  108.7 48.4 %shard_map.130 = bf16[4,1024,64]{2,1,0:T(8,128)(2,1)} custom-call(s32[1]{0:T(128)} %copy.74.len_ref, bf16[4,1024,64]{2,1,0:T(8,128)(2,1)} %maximum_bitcast_fusion.q_ref, bf16[4,4096,64]{2,1,0:T(8,128)(2,1)} %bitcast.60, bf16[4,4096,64]{2,1,0:T(8,128)(2,1)} %bitcast.61, bf16[4,1024,64]{2,1,0:T(8,128)(2,1)} %fusion.43.kn_ref, bf16[4,1024,64]{2,1,0:T(8,128)(2,1)} %bitcast.68), custom_call_target="tpu_custom_call" | custom-call | flops 5368709120 | bytes 6815744 | tf_op jit(solution)/shard_map/pallas_call | solution.py:151
  157.1 2.3 copy.61
  159.4 2.3 slice_bitcast_fusion.1
  161.8 1.5 copy.62
  163.3 4.3 %convolution_convert_fusion = bf16[1024,2048]{1,0:T(8,128)(2,1)} fusion(bf16[1024,256]{0,1:T(8,128)(2,1)} %bitcast.65, bf16[256,2048]{0,1:T(8,128)(2,1)S(1)} %bitcast.59), kind=kOutput, calls=%fused_computation.22 | convolution fusion | flops 1075838976 | bytes 5767168 | tf_op jit(solution)/shard_map/dot_general | solution.py:204
  167.6 0.0 reduce-scatter.2.cloned.1.call-start
  167.7 0.6 copy-done.9
  168.3 9.2 %fusion.34 = (bf16[16,1024,128]{2,1,0:T(8,128)(2,1)}, bf16[1024,16,128]{2,0,1:T(8,128)(2,1)}, bf16[16,1024,128]{2,1,0:T(8,128)(2,1)}) fusion(bf16[16,3328,128]{2,1,0:T(8,128)(2,1)} %bitcast.56), kind=kLoop, calls=%fused_computation.54 | loop fusion | bytes 25165824 | tf_op jit(solution)/shard_map/slice | solution.py:63
  177.5 7.3 %reshape_reshape.6 = bf16[2048,1024]{1,0:T(8,128)(2,1)} reshape(bf16[16,1024,128]{2,1,0:T(8,128)(2,1)} %get-tuple-element.16) | data formatting | bytes 8388608 | tf_op jit(solution)/shard_map/reshape;reshape | solution.py:67
  184.8 6.6 %copy.63 = bf16[1024,16,128]{0,2,1:T(8,128)(2,1)} copy(bf16[1024,16,128]{2,0,1:T(8,128)(2,1)} %get-tuple-element.15) | data formatting | bytes 8388608 | tf_op jit(solution)/shard_map/transpose | solution.py:64
  191.4 7.3 %reshape_reshape.7 = bf16[2048,1024]{1,0:T(8,128)(2,1)} reshape(bf16[16,1024,128]{2,1,0:T(8,128)(2,1)} %get-tuple-element.14) | data formatting | bytes 8388608 | tf_op jit(solution)/shard_map/reshape;reshape | solution.py:67
  198.8 51.5 %all-reduce.2.cloned.1.call-done = bf16[1024,2048]{1,0:T(8,128)(2,1)} async-done(((bf16[1024,2048]{1,0:T(8,128)(2,1)}), bf16[1024,2048]{1,0:T(8,128)(2,1)}) %all-reduce.2.cloned.1.call-update) | async-done | bytes 4194320 | tf_op jit(solution)/shard_map/psum | solution.py:207
  250.3 5.6 %fusion = (f32[1024]{0:T(1024)S(1)}, bf16[1024,2048]{1,0:T(8,128)(2,1)S(1)}) fusion(bf16[1024,2048]{1,0:T(8,128)(2,1)} %all-reduce.2.cloned.1.call-done, bf16[1024,2048]{1,0:T(8,128)(2,1)} %all-gather.4.cloned.1.call-done), kind=kLoop, calls=%fused_computation.5 | loop fusion | flops 14679040 | bytes 12587008 | tf_op jit(solution)/shard_map/reduce_sum | solution.py:19
  255.9 6.4 %fusion.25 = f32[1024,1024]{1,0:T(8,128)} fusion(bf16[2048,1024]{1,0:T(8,128)(2,1)S(1)} %copy-done.4, bf16[1024,2048]{1,0:T(8,128)(2,1)S(1)} %get-tuple-element.13, f32[2048]{0:T(1024)S(1)} %convert_element_type.80, f32[1024]{0:T(1024)S(1)} %add_rsqrt_fusion), kind=kOutput, calls=%fused_computation.37 | convolution fusion | flops 4303355904 | bytes 12595200 | tf_op jit(solution)/shard_map/dot_general | solution.py:213
  262.3 15.4 %convolution_convert_fusion.1 = bf16[1024,2048]{1,0:T(8,128)(2,1)} fusion(bf16[1024,2048]{0,1:T(8,128)(2,1)} %bitcast.62, f32[1024,1024]{1,0:T(8,128)} %fusion.25, bf16[2048,1024]{1,0:T(8,128)(2,1)} %reshape_reshape.7, bf16[1024,2048]{1,0:T(8,128)(2,1)} %copy-done.3, f32[2048]{0:T(1024)S(1)} %convert_element_type.80, f32[1024]{0:T(1024)S(1)} %add_rsqrt_fusion), kind=kOutput, calls=%fused_computation.23 | convolution fusion | flops 8606711808 | bytes 20983808 | tf_op jit(solution)/shard_map/dot_general | solution.py:222
  277.7 0.6 maximum_convert_fusion
  278.3 0.3 copy.64
  278.6 1.0 copy.65
  279.6 1.3 slice_bitcast_fusion.2
  280.9 1.0 copy.66
  281.9 33.9 %reduce-scatter.2.cloned.1.call-done = bf16[1024,256]{1,0:T(8,128)(2,1)} async-done(((bf16[1024,2048]{1,0:T(8,128)(2,1)}), bf16[1024,256]{1,0:T(8,128)(2,1)}) %reduce-scatter.2.cloned.1.call-update) | async-done | bytes 524304 | tf_op jit(solution)/shard_map/reduce_scatter | solution.py:225
  315.9 2.1 add_convert_fusion.1
  (33 shorter events, 0.1 us)
Async XLA Ops:
  7.2 5.0 %copy-start.7 = (bf16[3,128,256]{2,1,0:T(8,128)(2,1)S(1)}, bf16[3,128,256]{2,1,0:T(8,128)(2,1)}, u32[]{:S(2)}) copy-start(bf16[3,128,256]{2,1,0:T(8,128)(2,1)} %param.12) | copy-start | bytes 589828
  7.2 10.6 %copy-start.8 = (bf16[2048]{0:T(1024)(128)(2,1)S(1)}, bf16[2048]{0:T(1024)(128)(2,1)}, u32[]{:S(2)}) copy-start(bf16[2048]{0:T(1024)(128)(2,1)} %param.14) | copy-start | bytes 12292
  7.2 41.0 %all-gather.4.cloned.1.call-start = ((), (), s32[]{:S(2)}) async-start(), calls=%async_computation.1 | async-start | bytes 4718592 | tf_op jit(solution)/shard_map/all_gather | solution.py:175
  7.9 151.5 %all-gather.6.cloned.1.call-start = ((), (), s32[]{:S(2)}) async-start(), calls=%async_computation.4 | async-start | bytes 14483456 | tf_op jit(solution)/shard_map/all_gather | solution.py:58
  12.1 238.2 %all-reduce.2.cloned.1.call-start = ((), (), s32[]{:S(2)}) async-start(), calls=%async_computation.2 | async-start | bytes 8388608 | tf_op jit(solution)/shard_map/psum | solution.py:207
  12.3 20.4 %collective-permute-start = (bf16[3,128,256]{1,2,0:T(8,128)(2,1)S(1)}, bf16[3,128,256]{1,2,0:T(8,128)(2,1)S(1)}, u32[]{:S(2)}, u32[]{:S(2)}) collective-permute-start(bf16[3,128,256]{1,2,0:T(8,128)(2,1)S(1)} %copy.45), channel_id=1, source_target_pairs={{0,24},{8,0},{16,8},{24,16},{32,56},{40,32},{48,40},{56,48},{64,88... | collective-permute-start | bytes 589832 | tf_op jit(solution)/shard_map/ppermute | solution.py:48
  16.5 16.2 %collective-permute-start.1 = (bf16[3,128,256]{1,2,0:T(8,128)(2,1)S(1)}, bf16[3,128,256]{1,2,0:T(8,128)(2,1)}, u32[]{:S(2)}, u32[]{:S(2)}) collective-permute-start(bf16[3,128,256]{1,2,0:T(8,128)(2,1)S(1)} %copy.45), channel_id=1, source_target_pairs={{0,16},{8,24},{16,0},{24,8},{32,48},{40,56},{48,32},{56,40},{64,80... | collective-permute-start | bytes 589832 | tf_op jit(solution)/shard_map/ppermute | solution.py:48
  16.5 16.2 %collective-permute-start.2 = (bf16[3,128,256]{1,2,0:T(8,128)(2,1)S(1)}, bf16[3,128,256]{1,2,0:T(8,128)(2,1)}, u32[]{:S(2)}, u32[]{:S(2)}) collective-permute-start(bf16[3,128,256]{1,2,0:T(8,128)(2,1)S(1)} %copy.45), channel_id=1, source_target_pairs={{0,8},{8,16},{16,24},{24,0},{32,40},{40,48},{48,56},{56,32},{64,72... | collective-permute-start | bytes 589832 | tf_op jit(solution)/shard_map/ppermute | solution.py:48
  33.9 36.8 %collective-permute-start.3 = (bf16[3,4,128,256]{2,3,1,0:T(8,128)(2,1)S(1)}, bf16[3,4,128,256]{2,3,1,0:T(8,128)(2,1)}, u32[]{:S(2)}, u32[]{:S(2)}) collective-permute-start(bf16[3,4,128,256]{2,3,1,0:T(8,128)(2,1)S(1)} %get-tuple-element.28), channel_id=1, source_target_pairs={{0,96},{8,104},{16,112},{24,120},{32,0},{40,8},{48,16},{56,24},{64... | collective-permute-start | bytes 2359304 | tf_op jit(solution)/shard_map/ppermute | solution.py:50
  37.0 33.7 %collective-permute-start.4 = (bf16[3,4,128,256]{2,3,1,0:T(8,128)(2,1)S(1)}, bf16[3,4,128,256]{2,3,1,0:T(8,128)(2,1)}, u32[]{:S(2)}, u32[]{:S(2)}) collective-permute-start(bf16[3,4,128,256]{2,3,1,0:T(8,128)(2,1)S(1)} %get-tuple-element.28), channel_id=1, source_target_pairs={{0,64},{8,72},{16,80},{24,88},{32,96},{40,104},{48,112},{56,120},{... | collective-permute-start | bytes 2359304 | tf_op jit(solution)/shard_map/ppermute | solution.py:50
  37.6 43.9 %collective-permute-start.5 = (bf16[3,4,128,256]{2,3,1,0:T(8,128)(2,1)S(1)}, bf16[3,4,128,256]{2,3,1,0:T(8,128)(2,1)}, u32[]{:S(2)}, u32[]{:S(2)}) collective-permute-start(bf16[3,4,128,256]{2,3,1,0:T(8,128)(2,1)S(1)} %get-tuple-element.28), channel_id=1, source_target_pairs={{0,32},{8,40},{16,48},{24,56},{32,64},{40,72},{48,80},{56,88},{64,... | collective-permute-start | bytes 2359304 | tf_op jit(solution)/shard_map/ppermute | solution.py:50
  48.2 3.4 %copy-start = (bf16[1024,2048]{1,0:T(8,128)(2,1)S(1)}, bf16[1024,2048]{1,0:T(8,128)(2,1)}, u32[]{:S(2)}) copy-start(bf16[1024,2048]{1,0:T(8,128)(2,1)} %all-gather.4.cloned.1.call-done) | copy-start | bytes 12582916
  86.6 2.2 copy-start.5
  94.8 5.9 %copy-start.6 = (bf16[1,1024,256]{1,2,0:T(8,128)(2,1)S(1)}, bf16[1,1024,256]{1,2,0:T(8,128)(2,1)}, u32[]{:S(2)}) copy-start(bf16[1,1024,256]{1,2,0:T(8,128)(2,1)} %slice.58) | copy-start | bytes 1572868
  102.0 4.5 %copy-start.1 = (f32[1024,4,32]{2,0,1:T(8,128)S(1)}, f32[1024,4,32]{2,0,1:T(8,128)}, u32[]{:S(2)}) copy-start(f32[1024,4,32]{2,0,1:T(8,128)} %copy.69) | copy-start | bytes 1572868
  102.0 4.5 %copy-start.2 = (f32[1024,4,32]{2,0,1:T(8,128)S(1)}, f32[1024,4,32]{2,0,1:T(8,128)}, u32[]{:S(2)}) copy-start(f32[1024,4,32]{2,0,1:T(8,128)} %copy.70) | copy-start | bytes 1572868
  167.6 0.7 copy-start.9
  167.6 148.2 %reduce-scatter.2.cloned.1.call-start = ((), (), s32[]{:S(2)}) async-start(), calls=%async_computation.3 | async-start | bytes 4718592 | tf_op jit(solution)/shard_map/reduce_scatter | solution.py:225
  250.3 5.6 %copy-start.4 = (bf16[2048,1024]{1,0:T(8,128)(2,1)S(1)}, bf16[2048,1024]{1,0:T(8,128)(2,1)}, u32[]{:S(2)}) copy-start(bf16[2048,1024]{1,0:T(8,128)(2,1)} %reshape_reshape.6) | copy-start | bytes 12582916
  255.9 6.4 %copy-start.3 = (bf16[1024,2048]{1,0:T(8,128)(2,1)}, bf16[1024,2048]{1,0:T(8,128)(2,1)S(1)}, u32[]{:S(2)}) copy-start(bf16[1024,2048]{1,0:T(8,128)(2,1)S(1)} %get-tuple-element.13) | copy-start | bytes 12582916
Sparse Core Ops, SparseCore 0:
  9.7 38.4 all-gather.3
  50.4 102.6 all-gather.5
  167.7 82.4 all-reduce.1
  277.8 37.9 reduce-scatter.1

commit v6 on v5

--- a/solution.py
+++ b/solution.py
@@ -80,36 +80,40 @@
         l_sc[...] = jnp.zeros(l_sc.shape, jnp.float32)
         acc_sc[...] = jnp.zeros(acc_sc.shape, jnp.float32)
 
-    def update(k, v, mask):
-        s = lax.dot_general(q_ref[0], k, (((1,), (1,)), ((), ())), preferred_element_type=jnp.float32) * scale
-        if mask is not None:
+    def update(k, v, limit_of, chunk):
+        def one_chunk(index, carry):
+            rows = pl.ds(pl.multiple_of(index * chunk, chunk), chunk)
+            s = lax.dot_general(
+                q_ref[0, rows], k, (((1,), (1,)), ((), ())), preferred_element_type=jnp.float32
+            ) * scale
+            row = index * chunk + lax.broadcasted_iota(jnp.int32, s.shape, 0)
+            col = lax.broadcasted_iota(jnp.int32, s.shape, 1)
+            mask = col < limit_of(row)
             s = jnp.where(mask, s, NEG_FILL)
-        m_prev = m_sc[...]
-        m_new = jnp.maximum(m_prev, jnp.max(s, axis=1, keepdims=True))
-        alpha = jnp.exp(m_prev - m_new)
-        p = jnp.exp(s - m_new)
-        if mask is not None:
-            p = jnp.where(mask, p, 0.0)
-        l_sc[...] = alpha * l_sc[...] + jnp.sum(p, axis=1, keepdims=True)
-        acc_sc[...] = alpha * acc_sc[...] + jnp.dot(p.astype(jnp.bfloat16), v, preferred_element_type=jnp.float32)
-        m_sc[...] = m_new
+            m_prev = m_sc[rows]
+            m_new = jnp.maximum(m_prev, jnp.max(s, axis=1, keepdims=True))
+            alpha = jnp.exp(m_prev - m_new)
+            p = jnp.where(mask, jnp.exp(s - m_new), 0.0)
+            l_sc[rows] = alpha * l_sc[rows] + jnp.sum(p, axis=1, keepdims=True)
+            acc_sc[rows] = alpha * acc_sc[rows] + jnp.dot(
+                p.astype(jnp.bfloat16), v, preferred_element_type=jnp.float32
+            )
+            m_sc[rows] = m_new
+            return carry
+
+        lax.fori_loop(0, tq // chunk, one_chunk, 0)
 
     begin = j * tk
-
-    @pl.when((j < n_cache) & (begin + tk <= length))
+    in_cache = j < n_cache
+
+    @pl.when(jnp.logical_not(in_cache) | (begin < length))
     def _():
-        update(kc_ref[0], vc_ref[0], None)
-
-    @pl.when((j < n_cache) & (begin < length) & (begin + tk > length))
-    def _():
-        col = begin + lax.broadcasted_iota(jnp.int32, (tq, tk), 1)
-        update(kc_ref[0], vc_ref[0], col < length)
+        keys = jnp.where(in_cache, kc_ref[0], kn_ref[0])
+        values = jnp.where(in_cache, vc_ref[0], vn_ref[0])
+        update(keys, values, lambda row: jnp.where(in_cache, length - begin, row + 1), min(tq, 256))
 
     @pl.when(j == n_cache)
     def _():
-        row = lax.broadcasted_iota(jnp.int32, (tq, tq), 0)
-        col = lax.broadcasted_iota(jnp.int32, (tq, tq), 1)
-        update(kn_ref[0], vn_ref[0], row >= col)
         o_ref[0] = (acc_sc[...] / l_sc[...]).astype(o_ref.dtype)
 
 

time: 331 us -> 353 us (1.066); the launches traced: 325 us -> 351 us
  Pallas kernels: 48.4 us -> 69.4 us
  waiting for transfers between devices: 107 us -> 112 us
    pallas_call x1, Pallas kernels: 48.4 us -> 69.4 us  [flash_attention(): pl.pallas_call(body, grid_spec=grid_spec, out_shape=jax.ShapeDtypeStruct(...]
    psum x1, waiting for transfers between devices: 51.5 us -> 57.3 us  [on_device(): lax.psum(partial_value.astype(jnp.bfloat16), 'mp').astype(jnp.float32)]
  transfers between devices with their start and end apart: 10 -> 10, of which waited for: 4 -> 4; matrix products, arithmetic and copies ran while one was open for 33% -> 30% of each run, Pallas kernels for 15% -> 20%
where the time goes in v6:
time: 353 us; the launch traced here: 351 us
  waiting for transfers between devices  112 us (32%)
  local copies, waits for them, and re-layouts  83.3 us (24%)
  Pallas kernels  69.4 us (20%)
  matrix products  31.3 us (9%)
  other arithmetic  29.4 us (8%)
  between operations  14.6 us (4%)
  starting transfers between devices  10.5 us (3%)
    pallas_call x1, Pallas kernels, flash_attention(): pl.pallas_call(body, grid_spec=grid_spec, out_shape=jax.ShapeDtypeStruct(...  69.4 us
    psum x1, waiting for transfers between devices, on_device(): lax.psum(partial_value.astype(jnp.bfloat16), 'mp').astype(jnp.float32)  57.3 us
    reduce_scatter x1, waiting for transfers between devices, on_device(): lax.psum_scatter(terms.astype(jnp.bfloat16), 'mp', scatter_dimension=1, t...  33.9 us
    unnamed x29, local copies, waits for them, and re-layouts  19.7 us
    dot_general x1, matrix products, on_device(): terms = jnp.dot(units, w_down_full, preferred_element_type=jnp.float32)  15.4 us
    another operation x2, local copies, waits for them, and re-layouts, gather_packed(): outs.append(piece.reshape(shape))  14.7 us
    ppermute x3, waiting for transfers between devices, gather_req_shifted(): lax.ppermute(stage, axis_name, outer(k))  10.8 us
    transpose x3, local copies, waits for them, and re-layouts, gather_packed(): piece = jnp.moveaxis(piece, 0, axis)  10.3 us
  transfers between devices with their start and end apart: 10, of which 4 were waited for; matrix products, arithmetic and copies ran while one was open for 30% of the time, Pallas kernels for 20%

profile of v6, /device:TPU:0, one launch (start us, length us, event | category | flops | bytes accessed | tf_op | source)
XLA Modules:
  0.0 351.0 jit_solution(5851425141870985516)
XLA Ops:
  7.2 0.0 all-gather.4.cloned.1.call-start
  7.2 0.7 all-gather.4.cloned.1.call-update
  7.9 0.0 all-gather.6.cloned.1.call-start
  8.0 1.1 reshape.122
  9.0 1.1 reshape.123
  10.1 2.0 pad_maximum_fusion
  12.1 0.0 all-reduce.2.cloned.1.call-start
  12.1 0.2 copy.45
  12.3 4.2 %collective-permute-start = (bf16[3,128,256]{1,2,0:T(8,128)(2,1)S(1)}, bf16[3,128,256]{1,2,0:T(8,128)(2,1)S(1)}, u32[]{:S(2)}, u32[]{:S(2)}) collective-permute-start(bf16[3,128,256]{1,2,0:T(8,128)(2,1)S(1)} %copy.45), channel_id=1, source_target_pairs={{0,24},{8,0},{16,8},{24,16},{32,56},{40,32},{48,40},{56,48},{64,88... | collective-permute-start | bytes 589832 | tf_op jit(solution)/shard_map/ppermute | solution.py:48
  16.5 1.3 collective-permute-start.2
  18.4 3.0 copy.54
  21.4 3.2 copy.55
  24.6 2.9 copy.56
  27.5 3.2 copy.57
  30.8 1.9 multiply_cosine_fusion
  32.7 1.2 fusion.32
  33.9 3.1 collective-permute-start.3
  37.0 0.6 collective-permute-start.4
  37.6 1.0 collective-permute-start.5
  38.6 9.7 %all-gather.4.cloned.1.call-done = bf16[1024,2048]{1,0:T(8,128)(2,1)} async-done(((bf16[1024,256]{1,0:T(8,128)(2,1)}), bf16[1024,2048]{1,0:T(8,128)(2,1)}) %all-gather.4.cloned.1.call-update) | async-done | bytes 4194320 | tf_op jit(solution)/shard_map/all_gather | solution.py:179
  48.2 3.2 fusion.3
  51.5 0.2 copy-done
  51.7 3.1 fusion.5
  54.8 6.4 %copy.49 = bf16[1024,2048]{0,1:T(8,128)(2,1)} copy(bf16[1024,2048]{1,0:T(8,128)(2,1)} %fusion.5) | data formatting | bytes 8388608 | tf_op jit(solution)/shard_map/convert_element_type | solution.py:20
  61.2 6.3 %copy.50 = bf16[1024,4,4,128]{3,0,2,1:T(8,128)(2,1)} copy(bf16[1024,4,4,128]{0,3,2,1:T(8,128)(2,1)} %bitcast.54) | data formatting | bytes 8388608 | tf_op jit(solution)/shard_map/reshape | solution.py:181
  67.5 3.1 fusion.11
  70.7 10.8 %collective-permute-done.5 = bf16[3,4,128,256]{2,3,1,0:T(8,128)(2,1)} collective-permute-done((bf16[3,4,128,256]{2,3,1,0:T(8,128)(2,1)S(1)}, bf16[3,4,128,256]{2,3,1,0:T(8,128)(2,1)}, u32[]{:S(2)}, u32[]{:S(2)}) %collective-permute-start.5) | collective-permute-done | bytes 786464 | tf_op jit(solution)/shard_map/ppermute | solution.py:50
  81.5 5.2 %fusion.19 = f32[3,1024,256]{1,2,0:T(8,128)S(1)} fusion(s32[]{:T(128)S(6)} %select_n.41, bf16[1024,4,4,128]{3,0,2,1:T(8,128)(2,1)S(1)} %fusion.11, bf16[3,1,4,128,256]{3,4,2,0,1:T(8,128)(2,1)} %bitcast.7, bf16[3,1,4,128,256]{3,4,2,0,1:T(8,128)(2,1)} %bitcast.6, bf16[3,1,4,128,256]{3,4,2,0,1:T(8,128)(2,1)} %bitcast.5, ...), kind=kOutput, calls=%fused_computation.36 | convolution fusion | flops 3228041216 | bytes 10485764 | tf_op jit(solution)/shard_map/nd,kdw->knw/dot_general | solution.py:183
  86.7 1.0 slice.58
  87.6 0.1 fusion.35
  87.8 1.1 fusion.36
  88.8 3.0 copy.71
  91.8 3.0 copy.72
  94.8 0.9 fusion.37
  95.7 3.1 copy.69
  98.8 1.9 copy.70
  100.7 1.3 copy.60
  102.1 3.0 multiply_subtract_fusion
  105.0 1.6 fusion.43.kn_ref
  106.6 0.5 subtract_convert_fusion
  107.1 1.6 maximum_bitcast_fusion.q_ref
  108.7 69.4 %shard_map.130 = bf16[4,1024,64]{2,1,0:T(8,128)(2,1)} custom-call(s32[1]{0:T(128)} %copy.74.len_ref, bf16[4,1024,64]{2,1,0:T(8,128)(2,1)} %maximum_bitcast_fusion.q_ref, bf16[4,4096,64]{2,1,0:T(8,128)(2,1)} %bitcast.60, bf16[4,4096,64]{2,1,0:T(8,128)(2,1)} %bitcast.61, bf16[4,1024,64]{2,1,0:T(8,128)(2,1)} %fusion.43.kn_ref, bf16[4,1024,64]{2,1,0:T(8,128)(2,1)} %bitcast.68), custom_call_target="tpu_custom_call" | custom-call | flops 5368709120 | bytes 6815744 | tf_op jit(solution)/shard_map/pallas_call | solution.py:155
  178.1 2.3 copy.61
  180.5 2.3 slice_bitcast_fusion.1
  182.8 1.5 copy.62
  184.3 4.3 %convolution_convert_fusion = bf16[1024,2048]{1,0:T(8,128)(2,1)} fusion(bf16[1024,256]{0,1:T(8,128)(2,1)} %bitcast.65, bf16[256,2048]{0,1:T(8,128)(2,1)S(1)} %bitcast.59), kind=kOutput, calls=%fused_computation.22 | convolution fusion | flops 1075838976 | bytes 5767168 | tf_op jit(solution)/shard_map/dot_general | solution.py:208
  188.6 0.0 all-reduce.2.cloned.1.call-update
  188.6 0.3 reduce-scatter.2.cloned.1.call-start
  188.9 0.4 copy-done.9
  189.3 9.0 %fusion.34 = (bf16[16,1024,128]{2,1,0:T(8,128)(2,1)}, bf16[1024,16,128]{2,0,1:T(8,128)(2,1)}, bf16[16,1024,128]{2,1,0:T(8,128)(2,1)}) fusion(bf16[16,3328,128]{2,1,0:T(8,128)(2,1)} %bitcast.56), kind=kLoop, calls=%fused_computation.54 | loop fusion | bytes 25165824 | tf_op jit(solution)/shard_map/slice | solution.py:63
  198.3 7.3 %reshape_reshape.6 = bf16[2048,1024]{1,0:T(8,128)(2,1)} reshape(bf16[16,1024,128]{2,1,0:T(8,128)(2,1)} %get-tuple-element.16) | data formatting | bytes 8388608 | tf_op jit(solution)/shard_map/reshape;reshape | solution.py:67
  205.6 6.5 %copy.63 = bf16[1024,16,128]{0,2,1:T(8,128)(2,1)} copy(bf16[1024,16,128]{2,0,1:T(8,128)(2,1)} %get-tuple-element.15) | data formatting | bytes 8388608 | tf_op jit(solution)/shard_map/transpose | solution.py:64
  212.1 7.4 %reshape_reshape.7 = bf16[2048,1024]{1,0:T(8,128)(2,1)} reshape(bf16[16,1024,128]{2,1,0:T(8,128)(2,1)} %get-tuple-element.14) | data formatting | bytes 8388608 | tf_op jit(solution)/shard_map/reshape;reshape | solution.py:67
  219.5 57.3 %all-reduce.2.cloned.1.call-done = bf16[1024,2048]{1,0:T(8,128)(2,1)} async-done(((bf16[1024,2048]{1,0:T(8,128)(2,1)}), bf16[1024,2048]{1,0:T(8,128)(2,1)}) %all-reduce.2.cloned.1.call-update) | async-done | bytes 4194320 | tf_op jit(solution)/shard_map/psum | solution.py:211
  276.8 5.6 %fusion = (f32[1024]{0:T(1024)S(1)}, bf16[1024,2048]{1,0:T(8,128)(2,1)S(1)}) fusion(bf16[1024,2048]{1,0:T(8,128)(2,1)} %all-reduce.2.cloned.1.call-done, bf16[1024,2048]{1,0:T(8,128)(2,1)} %all-gather.4.cloned.1.call-done), kind=kLoop, calls=%fused_computation.5 | loop fusion | flops 14679040 | bytes 12587008 | tf_op jit(solution)/shard_map/reduce_sum | solution.py:19
  282.4 6.4 %fusion.25 = f32[1024,1024]{1,0:T(8,128)} fusion(bf16[2048,1024]{1,0:T(8,128)(2,1)S(1)} %copy-done.4, bf16[1024,2048]{1,0:T(8,128)(2,1)S(1)} %get-tuple-element.13, f32[2048]{0:T(1024)S(1)} %convert_element_type.80, f32[1024]{0:T(1024)S(1)} %add_rsqrt_fusion), kind=kOutput, calls=%fused_computation.37 | convolution fusion | flops 4303355904 | bytes 12595200 | tf_op jit(solution)/shard_map/dot_general | solution.py:217
  288.8 15.4 %convolution_convert_fusion.1 = bf16[1024,2048]{1,0:T(8,128)(2,1)} fusion(bf16[1024,2048]{0,1:T(8,128)(2,1)} %bitcast.62, f32[1024,1024]{1,0:T(8,128)} %fusion.25, bf16[2048,1024]{1,0:T(8,128)(2,1)} %reshape_reshape.7, bf16[1024,2048]{1,0:T(8,128)(2,1)} %copy-done.3, f32[2048]{0:T(1024)S(1)} %convert_element_type.80, f32[1024]{0:T(1024)S(1)} %add_rsqrt_fusion), kind=kOutput, calls=%fused_computation.23 | convolution fusion | flops 8606711808 | bytes 20983808 | tf_op jit(solution)/shard_map/dot_general | solution.py:226
  304.2 0.6 maximum_convert_fusion
  304.8 0.3 copy.64
  305.1 1.0 copy.65
  306.1 1.3 slice_bitcast_fusion.2
  307.4 1.0 copy.66
  308.4 33.9 %reduce-scatter.2.cloned.1.call-done = bf16[1024,256]{1,0:T(8,128)(2,1)} async-done(((bf16[1024,2048]{1,0:T(8,128)(2,1)}), bf16[1024,256]{1,0:T(8,128)(2,1)}) %reduce-scatter.2.cloned.1.call-update) | async-done | bytes 524304 | tf_op jit(solution)/shard_map/reduce_scatter | solution.py:229
  342.3 2.1 add_convert_fusion.1
  (33 shorter events, 0.1 us)
Async XLA Ops:
  7.2 5.0 %copy-start.7 = (bf16[3,128,256]{2,1,0:T(8,128)(2,1)S(1)}, bf16[3,128,256]{2,1,0:T(8,128)(2,1)}, u32[]{:S(2)}) copy-start(bf16[3,128,256]{2,1,0:T(8,128)(2,1)} %param.12) | copy-start | bytes 589828
  7.2 10.6 %copy-start.8 = (bf16[2048]{0:T(1024)(128)(2,1)S(1)}, bf16[2048]{0:T(1024)(128)(2,1)}, u32[]{:S(2)}) copy-start(bf16[2048]{0:T(1024)(128)(2,1)} %param.14) | copy-start | bytes 12292
  7.2 41.0 %all-gather.4.cloned.1.call-start = ((), (), s32[]{:S(2)}) async-start(), calls=%async_computation.1 | async-start | bytes 4718592 | tf_op jit(solution)/shard_map/all_gather | solution.py:179
  7.9 172.5 %all-gather.6.cloned.1.call-start = ((), (), s32[]{:S(2)}) async-start(), calls=%async_computation.4 | async-start | bytes 14483456 | tf_op jit(solution)/shard_map/all_gather | solution.py:58
  12.1 264.7 %all-reduce.2.cloned.1.call-start = ((), (), s32[]{:S(2)}) async-start(), calls=%async_computation.2 | async-start | bytes 8388608 | tf_op jit(solution)/shard_map/psum | solution.py:211
  12.3 20.4 %collective-permute-start = (bf16[3,128,256]{1,2,0:T(8,128)(2,1)S(1)}, bf16[3,128,256]{1,2,0:T(8,128)(2,1)S(1)}, u32[]{:S(2)}, u32[]{:S(2)}) collective-permute-start(bf16[3,128,256]{1,2,0:T(8,128)(2,1)S(1)} %copy.45), channel_id=1, source_target_pairs={{0,24},{8,0},{16,8},{24,16},{32,56},{40,32},{48,40},{56,48},{64,88... | collective-permute-start | bytes 589832 | tf_op jit(solution)/shard_map/ppermute | solution.py:48
  16.5 16.2 %collective-permute-start.1 = (bf16[3,128,256]{1,2,0:T(8,128)(2,1)S(1)}, bf16[3,128,256]{1,2,0:T(8,128)(2,1)}, u32[]{:S(2)}, u32[]{:S(2)}) collective-permute-start(bf16[3,128,256]{1,2,0:T(8,128)(2,1)S(1)} %copy.45), channel_id=1, source_target_pairs={{0,16},{8,24},{16,0},{24,8},{32,48},{40,56},{48,32},{56,40},{64,80... | collective-permute-start | bytes 589832 | tf_op jit(solution)/shard_map/ppermute | solution.py:48
  16.5 16.2 %collective-permute-start.2 = (bf16[3,128,256]{1,2,0:T(8,128)(2,1)S(1)}, bf16[3,128,256]{1,2,0:T(8,128)(2,1)}, u32[]{:S(2)}, u32[]{:S(2)}) collective-permute-start(bf16[3,128,256]{1,2,0:T(8,128)(2,1)S(1)} %copy.45), channel_id=1, source_target_pairs={{0,8},{8,16},{16,24},{24,0},{32,40},{40,48},{48,56},{56,32},{64,72... | collective-permute-start | bytes 589832 | tf_op jit(solution)/shard_map/ppermute | solution.py:48
  33.9 36.8 %collective-permute-start.3 = (bf16[3,4,128,256]{2,3,1,0:T(8,128)(2,1)S(1)}, bf16[3,4,128,256]{2,3,1,0:T(8,128)(2,1)}, u32[]{:S(2)}, u32[]{:S(2)}) collective-permute-start(bf16[3,4,128,256]{2,3,1,0:T(8,128)(2,1)S(1)} %get-tuple-element.28), channel_id=1, source_target_pairs={{0,96},{8,104},{16,112},{24,120},{32,0},{40,8},{48,16},{56,24},{64... | collective-permute-start | bytes 2359304 | tf_op jit(solution)/shard_map/ppermute | solution.py:50
  37.0 33.7 %collective-permute-start.4 = (bf16[3,4,128,256]{2,3,1,0:T(8,128)(2,1)S(1)}, bf16[3,4,128,256]{2,3,1,0:T(8,128)(2,1)}, u32[]{:S(2)}, u32[]{:S(2)}) collective-permute-start(bf16[3,4,128,256]{2,3,1,0:T(8,128)(2,1)S(1)} %get-tuple-element.28), channel_id=1, source_target_pairs={{0,64},{8,72},{16,80},{24,88},{32,96},{40,104},{48,112},{56,120},{... | collective-permute-start | bytes 2359304 | tf_op jit(solution)/shard_map/ppermute | solution.py:50
  37.6 43.9 %collective-permute-start.5 = (bf16[3,4,128,256]{2,3,1,0:T(8,128)(2,1)S(1)}, bf16[3,4,128,256]{2,3,1,0:T(8,128)(2,1)}, u32[]{:S(2)}, u32[]{:S(2)}) collective-permute-start(bf16[3,4,128,256]{2,3,1,0:T(8,128)(2,1)S(1)} %get-tuple-element.28), channel_id=1, source_target_pairs={{0,32},{8,40},{16,48},{24,56},{32,64},{40,72},{48,80},{56,88},{64,... | collective-permute-start | bytes 2359304 | tf_op jit(solution)/shard_map/ppermute | solution.py:50
  48.2 3.4 copy-start
  86.6 2.2 copy-start.5
  94.8 5.9 %copy-start.6 = (bf16[1,1024,256]{1,2,0:T(8,128)(2,1)S(1)}, bf16[1,1024,256]{1,2,0:T(8,128)(2,1)}, u32[]{:S(2)}) copy-start(bf16[1,1024,256]{1,2,0:T(8,128)(2,1)} %slice.58) | copy-start | bytes 1572868
  102.0 4.5 %copy-start.1 = (f32[1024,4,32]{2,0,1:T(8,128)S(1)}, f32[1024,4,32]{2,0,1:T(8,128)}, u32[]{:S(2)}) copy-start(f32[1024,4,32]{2,0,1:T(8,128)} %copy.69) | copy-start | bytes 1572868
  102.0 4.5 %copy-start.2 = (f32[1024,4,32]{2,0,1:T(8,128)S(1)}, f32[1024,4,32]{2,0,1:T(8,128)}, u32[]{:S(2)}) copy-start(f32[1024,4,32]{2,0,1:T(8,128)} %copy.70) | copy-start | bytes 1572868
  188.6 0.7 copy-start.9
  188.6 153.7 %reduce-scatter.2.cloned.1.call-start = ((), (), s32[]{:S(2)}) async-start(), calls=%async_computation.3 | async-start | bytes 4718592 | tf_op jit(solution)/shard_map/reduce_scatter | solution.py:229
  276.8 5.6 %copy-start.4 = (bf16[2048,1024]{1,0:T(8,128)(2,1)S(1)}, bf16[2048,1024]{1,0:T(8,128)(2,1)}, u32[]{:S(2)}) copy-start(bf16[2048,1024]{1,0:T(8,128)(2,1)} %reshape_reshape.6) | copy-start | bytes 12582916
  282.4 6.4 %copy-start.3 = (bf16[1024,2048]{1,0:T(8,128)(2,1)}, bf16[1024,2048]{1,0:T(8,128)(2,1)S(1)}, u32[]{:S(2)}) copy-start(bf16[1024,2048]{1,0:T(8,128)(2,1)S(1)} %get-tuple-element.13) | copy-start | bytes 12582916
Sparse Core Ops, SparseCore 0:
  9.7 38.4 all-gather.3
  50.4 102.6 all-gather.5
  188.8 87.9 all-reduce.1
  304.3 37.9 reduce-scatter.1
